TPU v7x, 128 devices: a whole 4x4x4 slice. The times are simulated.
128 devices in a mesh: seq: 16 (over z, x), head: 8 (over y, core).
Axes of the slice: x: 4, y: 4, z: 4, core: 2. Of those that a mesh axis runs over, the one named last changes fastest.
Arguments:
- inputs: bfloat16 [16384, 8192], P('seq', 'head'), as said below
- gate_input: bfloat16 [16384, 8192], P('seq', 'head'), may hold values from -6 to 6
- log_decay: float32 [16384, 128], P('seq', 'head'), as said below
- b_matrix: bfloat16 [16384, 8, 128], P('seq', 'head'), may hold values from -6 to 6
- c_matrix: bfloat16 [16384, 8, 128], P('seq', 'head'), may hold values from -1.25 to 1.25
- norm_gain: float32 [8192], P('head'), may hold values from 0.1 to 1.9
- cotangent: bfloat16 [16384, 8192], P('seq', 'head'), may hold values from -6 to 6
Outputs:
- normed: bfloat16 [16384, 8192], P('seq', 'head')
- grad_inputs: bfloat16 [16384, 8192], P('seq', 'head')
- grad_gate: bfloat16 [16384, 8192], P('seq', 'head')
- grad_decay: float32 [16384, 128], P('seq', 'head')
- grad_b_matrix: float32 [16384, 8, 128], P('seq', 'head')
- grad_c_matrix: float32 [16384, 8, 128], P('seq', 'head')
Inputs may be any that keep to these rules, and one draw needn't show every extreme that they name: `log_decay`: every entry is strictly negative. `inputs`: real-valued and finite.
All inputs are finite; a program needn't handle non-finite values.
Results may differ from a plain program's by a relative error of at most 0.003.
Values sent between devices are 32-bit elements; how exact they have to be, the bound alone decides.
No kernel may reach another device: no remote copies, remote signals or barrier semaphores. Data moves between devices by JAX's collectives and lax.ppermute only.
A program may use at most 192 MiB of HBM per device.

v0:
```python
import jax
import jax.numpy as jnp
from jax import lax
from jax.sharding import PartitionSpec as P


SPAN = 128


PRECISION = lax.Precision.HIGH
EXACT = lax.Precision.HIGHEST
EPSILON = 1e-05


ROW = 4


def gap_weights(log_carry, place, later, ids=None):
    if ids is None:
        ids = jnp.arange(log_carry.shape[0])
    if later:
        source_ok = ids > place
        between = (ids[None, :] > place) & (ids[None, :] < ids[:, None])
    else:
        source_ok = ids < place
        between = (ids[None, :] > ids[:, None]) & (ids[None, :] < place)
    log_gap = jnp.sum(jnp.where(between[:, :, None, None], log_carry[None], 0.0), axis=1)
    return jnp.where(source_ok[:, None, None], jnp.exp(log_gap), 0.0)


def tile_logs(log_carry, like):
    return jnp.broadcast_to(log_carry[..., None, None], like.shape[:2] + (8, like.shape[3]))


def grouped_gather(value, groups, place):
    size = len(groups[0])
    parts = [value]
    for shift in range(1, size):
        pairs = [(g[k], g[(k + shift) % size]) for g in groups for k in range(size)]
        parts.append(lax.ppermute(value, "seq", pairs))
    sources = (place - jnp.arange(size)) % size
    return jnp.stack(parts), sources


def seq_groups():
    count = lax.axis_size("seq")
    rows = count // ROW
    row_groups = [[z * ROW + x for x in range(ROW)] for z in range(rows)]
    col_groups = [[z * ROW + x for z in range(rows)] for x in range(ROW)]
    return row_groups, col_groups


def prefix_state(final, log_carry):
    place = lax.axis_index("seq")
    col, row = place % ROW, place // ROW
    row_groups, col_groups = seq_groups()
    size = final.shape[2]
    row_all, row_ids = grouped_gather(
        jnp.concatenate([final, tile_logs(log_carry, final)], axis=2), row_groups, col
    )
    row_logs = jnp.max(row_all[:, :, :, size:], axis=(3, 4))
    in_row = weighted_sum(gap_weights(row_logs, col, False, row_ids), row_all)[:, :, :size]
    row_total = weighted_sum(gap_weights(row_logs, ROW, False, row_ids), row_all)[:, :, :size]
    row_log = jnp.sum(row_logs, axis=0)
    col_all, col_ids = grouped_gather(
        jnp.concatenate([row_total, tile_logs(row_log, final)], axis=2), col_groups, row
    )
    col_logs = jnp.max(col_all[:, :, :, size:], axis=(3, 4))
    before_row = weighted_sum(gap_weights(col_logs, row, False, col_ids), col_all)[:, :, :size]
    into_row = jnp.sum(jnp.where((row_ids < col)[:, None, None], row_logs, 0.0), axis=0)
    incoming = in_row + jnp.exp(into_row)[..., None, None] * before_row
    return incoming, (row_logs, row_ids, col_logs, col_ids)


def suffix_state(leaving, logs):
    row_logs, row_ids, col_logs, col_ids = logs
    place = lax.axis_index("seq")
    col, row = place % ROW, place // ROW
    row_groups, col_groups = seq_groups()
    row_all = grouped_gather(leaving, row_groups, col)[0]
    in_row = weighted_sum(gap_weights(row_logs, col, True, row_ids), row_all)
    row_head = weighted_sum(gap_weights(row_logs, -1, True, row_ids), row_all)
    col_all = grouped_gather(row_head, col_groups, row)[0]
    after_row = weighted_sum(gap_weights(col_logs, row, True, col_ids), col_all)
    out_of_row = jnp.sum(jnp.where((row_ids > col)[:, None, None], row_logs, 0.0), axis=0)
    return in_row + jnp.exp(out_of_row)[..., None, None] * after_row


def head_sum(values):
    count = lax.axis_size("head")
    if count & (count - 1):
        return lax.psum(values, "head")
    shift = 1
    while shift < count:
        pairs = [(i, i ^ shift) for i in range(count)]
        values = values + lax.ppermute(values, "head", pairs)
        shift *= 2
    return values


def weighted_sum(weights, states):
    total = weights[0][..., None, None] * states[0]
    for source in range(1, states.shape[0]):
        total = total + weights[source][..., None, None] * states[source]
    return total


def pair_scores(c_half, b_half):
    return jnp.einsum("kign,kjgn->kgij", c_half, b_half, preferred_element_type=jnp.float32)


def score_grads(grad_scores, b_blocks, c_blocks):
    grad_c = jnp.einsum("kgij,kjgn->kign", grad_scores, b_blocks, precision=PRECISION)
    grad_b = jnp.einsum("kgij,kign->kjgn", grad_scores, c_blocks, precision=PRECISION)
    return (grad_b, grad_c)


def block_chain(x_blocks, a_blocks, b_blocks):
    length = a_blocks.shape[1]
    ids = jnp.arange(length)
    lower = (ids[:, None] >= ids[None, :]).astype(jnp.float32)
    running = jnp.einsum("kjgr,ij->kgri", a_blocks, lower, precision=EXACT)
    span_end = running[..., -1]
    to_end = jnp.exp(span_end[..., None] - running)
    scaled = x_blocks * jnp.moveaxis(to_end, 3, 1)[..., None]
    block_states = jnp.einsum("kjgrp,kjgn->kgrpn", scaled, b_blocks, precision=PRECISION)
    factors = jnp.exp(span_end)
    carried = jnp.zeros(block_states.shape[1:], jnp.float32)
    start_list = []
    for block in range(block_states.shape[0]):
        start_list.append(carried)
        carried = factors[block][..., None, None] * carried + block_states[block]
    return (running, span_end, jnp.stack(start_list), carried)


def local_core(x_blocks, a_blocks, b_blocks, c_blocks, scores):
    running, span_end, starts, _ = block_chain(x_blocks, a_blocks, b_blocks)
    length = running.shape[3]
    row_numbers = lax.broadcasted_iota(jnp.int32, (length, length), 0)
    col_ids = lax.broadcasted_iota(jnp.int32, (length, length), 1)
    causal = row_numbers >= col_ids
    log_gaps = running[..., :, None] - running[..., None, :]
    decays = jnp.exp(jnp.where(causal, log_gaps, -1e30))
    weighted = decays * scores[:, :, None]
    diagonal = jnp.einsum("kgrij,kjgrp->kigrp", weighted, x_blocks, precision=PRECISION)
    from_state = jnp.einsum("kign,kgrpn->kigrp", c_blocks, starts, precision=PRECISION)
    ssd_part = diagonal + from_state * jnp.moveaxis(jnp.exp(running), 3, 1)[..., None]
    earlier = jnp.cumsum(span_end, axis=0) - span_end
    reach = jnp.exp(running + earlier[..., None])
    return (ssd_part, reach)


def edge_grads(adjoint, carry_grad, x_blocks, b_blocks, to_end, later, carry_all):
    tokens = x_blocks.shape[0] * x_blocks.shape[1]
    x_tok = x_blocks.reshape((tokens,) + x_blocks.shape[2:])
    b_tok = b_blocks.reshape((tokens,) + b_blocks.shape[2:])
    weights = jnp.exp(jnp.moveaxis(to_end + later[..., None], 3, 1))
    weights = weights.reshape((tokens,) + weights.shape[2:])
    projected = jnp.einsum("tgn,grpn->tgrp", b_tok, adjoint, precision=PRECISION)
    grad_x = weights[..., None] * projected
    log_grad = weights * jnp.sum(x_tok * projected, axis=3)
    grad_b = jnp.einsum("tgrp,grpn->tgn", weights[..., None] * x_tok, adjoint, precision=PRECISION)
    ids = jnp.arange(tokens)
    strict = (ids[:, None] > ids[None, :]).astype(jnp.float32)
    before = jnp.einsum("tgr,st->sgr", log_grad, strict, precision=EXACT)
    grad_a = before + (carry_grad * carry_all)[None]
    return (
        grad_x.reshape(x_blocks.shape),
        grad_a.reshape(x_blocks.shape[:4]),
        grad_b.reshape(b_blocks.shape),
    )


def add_incoming(ssd_part, reach, c_blocks, incoming):
    projected = jnp.einsum("kign,grpn->kigrp", c_blocks, incoming, precision=PRECISION)
    return ssd_part + projected * jnp.moveaxis(reach, 3, 1)[..., None]


def device_body(inputs, gate_input, log_decay, b_matrix, c_matrix, norm_gain, cotangent):
    tok_rows, width = inputs.shape
    head_count = log_decay.shape[1]
    groups = b_matrix.shape[1]
    state_size = b_matrix.shape[2]
    head_size = width // head_count
    per_group = head_count // groups
    blocks = tok_rows // SPAN
    full_width = width * lax.axis_size("head")
    x_blocks = inputs.astype(jnp.float32).reshape(blocks, SPAN, groups, per_group, head_size)
    a_blocks = log_decay.reshape(blocks, SPAN, groups, per_group)
    b_half = b_matrix.reshape(blocks, SPAN, groups, state_size)
    c_half = c_matrix.reshape(blocks, SPAN, groups, state_size)
    b_blocks = b_half.astype(jnp.float32)
    c_blocks = c_half.astype(jnp.float32)
    scores = pair_scores(c_half, b_half)
    core_out, core_pull = jax.vjp(local_core, x_blocks, a_blocks, b_blocks, c_blocks, scores)
    ssd_part, reach = core_out
    ssd_part = lax.optimization_barrier(ssd_part)
    running, span_end, _, _ = block_chain(x_blocks, a_blocks, b_blocks)
    carry_all = jnp.exp(jnp.sum(span_end, axis=0))
    to_end = span_end[..., None] - running
    later = jnp.cumsum(span_end[::-1], axis=0)[::-1] - span_end
    token_weights = jnp.exp(jnp.moveaxis(to_end + later[..., None], 3, 1)).reshape(
        tok_rows, groups, per_group
    )
    weighted_x = inputs.astype(jnp.float32).reshape(tok_rows, groups, per_group, head_size)
    final = jnp.einsum(
        "tgrp,tgn->grpn",
        weighted_x * token_weights[..., None],
        b_matrix.astype(jnp.float32),
        precision=PRECISION,
    )
    log_carry = jnp.sum(a_blocks, axis=(0, 1))
    incoming, seq_logs = prefix_state(final, log_carry)

    def light_step(part_a, part_b, part_c):
        return add_incoming(part_a, part_b, part_c, incoming)

    light_out, light_pull = jax.vjp(light_step, ssd_part, reach, c_blocks)
    ssd_out = light_out.reshape(tok_rows, width)
    gate_value = gate_input.astype(jnp.float32)
    sigmoid_gate = jax.nn.sigmoid(gate_value)
    gate_silu = gate_value * sigmoid_gate
    scaled_cot = norm_gain[None, :] * cotangent.astype(jnp.float32)
    gated = ssd_out * gate_silu
    squares, products = head_sum(
        jnp.stack([jnp.sum(gated * gated, axis=1), jnp.sum(gated * scaled_cot, axis=1)])
    )
    inverse_rms = lax.rsqrt(squares / full_width + EPSILON)
    normed = (gated * inverse_rms[:, None] * norm_gain[None, :]).astype(jnp.bfloat16)
    grad_gated = (
        inverse_rms[:, None] * scaled_cot
        - gated * (inverse_rms**3 * products / full_width)[:, None]
    )
    grad_gate = (
        grad_gated * ssd_out * sigmoid_gate * (1.0 + gate_value * (1.0 - sigmoid_gate))
    ).astype(jnp.bfloat16)
    grad_ssd = grad_gated * gate_silu
    upstream = grad_ssd.reshape(blocks, SPAN, groups, per_group, head_size)
    reached = upstream * jnp.moveaxis(reach, 3, 1)[..., None]
    leaving = jnp.einsum("kign,kigrp->grpn", c_blocks, reached, precision=PRECISION)
    adjoint = suffix_state(leaving, seq_logs)
    light_grads = light_pull(upstream)
    core_grads = lax.optimization_barrier(core_pull(tuple(light_grads[:2])))
    carry_grad = jnp.sum(adjoint * incoming, axis=(2, 3))
    edge_x, edge_a, edge_b = edge_grads(
        adjoint, carry_grad, x_blocks, b_blocks, to_end, later, carry_all
    )
    grad_x_core, grad_a_core, grad_b_core, grad_c_core, grad_scores = core_grads
    extra_b, extra_c = score_grads(grad_scores, b_blocks, c_blocks)
    grad_x = grad_x_core + edge_x
    grad_a = grad_a_core + edge_a
    grad_b = grad_b_core + extra_b + edge_b
    grad_c = grad_c_core + extra_c + light_grads[2]
    grad_inputs = grad_x.reshape(tok_rows, width).astype(jnp.bfloat16)
    grad_decay = grad_a.reshape(tok_rows, head_count)
    grad_b_matrix = grad_b.reshape(tok_rows, groups, state_size)
    grad_c_matrix = grad_c.reshape(tok_rows, groups, state_size)
    return (normed, grad_inputs, grad_gate, grad_decay, grad_b_matrix, grad_c_matrix)


def solution(mesh):
    placed = (
        P("seq", "head"),
        P("seq", "head"),
        P("seq", "head"),
        P("seq", "head", None),
        P("seq", "head", None),
        P("head"),
        P("seq", "head"),
    )
    return jax.shard_map(
        device_body,
        mesh=mesh,
        in_specs=placed,
        out_specs=(
            P("seq", "head"),
            P("seq", "head"),
            P("seq", "head"),
            P("seq", "head"),
            P("seq", "head", None),
            P("seq", "head", None),
        ),
        check_vma=False,
    )
```

profile of v0, /device:TPU:1, one launch (start us, length us, event | category | flops | bytes accessed | tf_op | source)
XLA Modules:
  0.0 236.1 jit_solution(14752836579490268599)
XLA Ops:
  4.6 2.9 %copy.80 = bf16[1024,1024]{0,1:T(8,128)(2,1)S(1)} copy(bf16[1024,1024]{1,0:T(8,128)(2,1)} %param.7) | data formatting | bytes 4194304 | tf_op args[0]
  8.4 1.3 convolution_bitcast_fusion.2
  9.8 1.1 fusion.163
  10.9 2.0 collective-permute-start
  12.9 2.5 %collective-permute-start.1 = (f32[1,16,72,128]{3,2,1,0:T(8,128)}, f32[1,16,72,128]{3,2,1,0:T(8,128)}, u32[]{:S(2)}, u32[]{:S(2)}) collective-permute-start(f32[1,16,72,128]{3,2,1,0:T(8,128)} %get-tuple-element.89), channel_id=1, source_target_pairs={{0,16},{8,24},{16,0},{24,8},{32,48},{40,56},{48,32},{56,40},{64,80... | collective-permute-start | bytes 1769480 | tf_op jit(solution)/shard_map/ppermute | solution.py:40
  15.4 1.3 collective-permute-start.2
  18.3 4.3 %fusion.165 = (f32[1024,1024]{0,1:T(8,128)}, f32[128,8,8,128]{3,1,2,0:T(8,128)}) fusion(bf16[1024,1024]{0,1:T(8,128)(2,1)S(1)} %copy.80), kind=kLoop, calls=%fused_computation.310 | loop fusion | flops 1048576 | bytes 10485760 | tf_op jit(solution)/shard_map/convert_element_type | solution.py:188
  23.6 5.2 %copy.137 = f32[128,8,8,128]{3,2,1,0:T(8,128)} copy(f32[128,8,8,128]{3,1,2,0:T(8,128)} %get-tuple-element.85) | data formatting | bytes 8388608
  28.9 1.9 copy.136
  30.8 2.6 %broadcast_multiply_fusion.1 = f32[8,128,16,64]{1,0,3,2:T(8,128)S(1)} fusion(f32[8,128,16,64]{1,0,3,2:T(8,128)} %bitcast.583, f32[8,128,16]{1,0,2:T(8,128)S(1)} %copy.83), kind=kLoop, calls=%fused_computation.91 | loop fusion | flops 1048576 | bytes 8454144 | tf_op jit(solution)/shard_map/jvp()/mul | solution.py:125
  33.4 1.6 fusion.53
  35.5 3.1 %copy-done.6 = f32[8,1,16,64,128]{4,3,2,1,0:T(8,128)S(1)} copy-done((f32[8,1,16,64,128]{4,3,2,1,0:T(8,128)S(1)}, f32[8,1,16,64,128]{4,3,2,1,0:T(8,128)}, u32[]{:S(2)}) %copy-start.6) | copy-done | bytes 4194328
  41.0 1.4 fusion.30
  44.1 7.8 %bitcast_add_fusion.1 = f32[8,128,1,16,64]{1,4,3,0,2:T(8,128)} fusion(f32[8,16,64,128]{3,2,1,0:T(8,128)S(1)} %fusion.30, f32[8,128,16]{1,2,0:T(8,128)S(1)} %get-tuple-element.93, f32[8,128,128]{2,1,0:T(8,128)S(1)} %fusion.168, f32[8,16,128]{2,1,0:T(8,128)S(1)} %bitcast.593, pred[128,128]{1,0:T(8,128)(4,1)S(1)} %iota_compare_fusion.6, ...), kind=kOutput, calls=%fused_computation.23 | convolution fusion | flops 813694976 | bytes 11157504 | tf_op jit(solution)/shard_map/jvp(kgrij,kjgrp->kigrp)/dot_general | solution.py:145
  52.5 2.9 %copy.88 = bf16[1024,1024]{0,1:T(8,128)(2,1)S(1)} copy(bf16[1024,1024]{1,0:T(8,128)(2,1)} %param.8) | data formatting | bytes 4194304 | tf_op args[1]
  55.4 3.9 %copy.89 = bf16[1024,1024]{0,1:T(8,128)(2,1)} copy(bf16[1024,1024]{1,0:T(8,128)(2,1)} %param.13) | data formatting | bytes 4194304 | tf_op args[6]
  59.3 1.5 copy.106
  60.8 1.3 compare_and_fusion.5
  62.1 1.3 compare_and_fusion.3
  63.5 1.1 fusion.120
  66.1 1.6 multiply_add_fusion
  67.8 1.7 collective-permute-start.3
  69.5 3.3 %collective-permute-start.4 = (f32[1,16,72,128]{3,2,1,0:T(8,128)S(1)}, f32[1,16,72,128]{3,2,1,0:T(8,128)S(1)}, u32[]{:S(2)}, u32[]{:S(2)}) collective-permute-start(f32[1,16,72,128]{3,2,1,0:T(8,128)S(1)} %get-tuple-element.87), channel_id=1, source_target_pairs={{0,64},{32,96},{64,0},{96,32},{8,72},{40,104},{72,8},{104,40},{16,... | collective-permute-start | bytes 1769480 | tf_op jit(solution)/shard_map/ppermute | solution.py:40
  75.8 8.0 %collective-permute-done.3 = f32[1,16,72,128]{3,2,1,0:T(8,128)S(1)} collective-permute-done((f32[1,16,72,128]{3,2,1,0:T(8,128)S(1)}, f32[1,16,72,128]{3,2,1,0:T(8,128)S(1)}, u32[]{:S(2)}, u32[]{:S(2)}) %collective-permute-start.3) | collective-permute-done | bytes 589856 | tf_op jit(solution)/shard_map/ppermute | solution.py:40
  83.8 13.5 %collective-permute-done.4 = f32[1,16,72,128]{3,2,1,0:T(8,128)S(1)} collective-permute-done((f32[1,16,72,128]{3,2,1,0:T(8,128)S(1)}, f32[1,16,72,128]{3,2,1,0:T(8,128)S(1)}, u32[]{:S(2)}, u32[]{:S(2)}) %collective-permute-start.4) | collective-permute-done | bytes 589856 | tf_op jit(solution)/shard_map/ppermute | solution.py:40
  98.1 1.7 fusion.102
  99.9 1.6 fusion.23
  101.5 3.3 %copy.87 = f32[8,128,1,16,64]{1,0,4,3,2:T(8,128)S(1)} copy(f32[8,128,1,16,64]{1,4,3,0,2:T(8,128)S(1)} %get-tuple-element.139) | data formatting | bytes 8388608 | tf_op jit(solution)/shard_map/jvp()/add | solution.py:176
  104.9 2.8 %multiply_reduce_fusion.2 = (f32[1024]{0:T(1024)S(1)}, f32[1024]{0:T(1024)S(1)}) fusion(bf16[1024,1024]{0,1:T(8,128)(2,1)S(1)} %copy.88, f32[128,8,8,128]{3,2,1,0:T(8,128)S(1)} %bitcast.579, bf16[1024,1024]{0,1:T(8,128)(2,1)S(1)} %copy-done.9, f32[1024]{0:T(1024)S(1)} %copy-done.52), kind=kLoop, calls=%fused_computation.63 | loop fusion | flops 12580864 | bytes 8400896 | tf_op jit(solution)/shard_map/reduce_sum | solution.py:226
  107.7 2.1 collective-permute-start.6
  111.0 1.4 collective-permute-start.7
  112.4 1.1 collective-permute-done.7
  113.6 3.0 %collective-permute-start.8 = (f32[2,1024]{1,0:T(2,128)S(1)}, f32[2,1024]{1,0:T(2,128)S(1)}, u32[]{:S(2)}, u32[]{:S(2)}) collective-permute-start(f32[2,1024]{1,0:T(2,128)S(1)} %fusion.181), channel_id=1, source_target_pairs={{0,4},{1,5},{2,6},{3,7},{4,0},{5,1},{6,2},{7,3},{8,12},{9,13},{10,... | collective-permute-start | bytes 24584 | tf_op jit(solution)/shard_map/ppermute | solution.py:96
  117.7 5.0 %fusion.12 = (bf16[1024,1024]{0,1:T(8,128)(2,1)}, f32[128,8,8,128]{3,1,2,0:T(8,128)S(1)}, bf16[1024,1024]{0,1:T(8,128)(2,1)}) fusion(bf16[1024,1024]{0,1:T(8,128)(2,1)S(1)} %copy.88, f32[128,8,8,128]{3,2,1,0:T(8,128)S(1)} %bitcast.580, bf16[1024,1024]{0,1:T(8,128)(2,1)S(1)} %copy-done.9, f32[1024]{0:T(1024)S(1)} %fusion.148, f32[1024]{0:T(1024)S(1)} %bitcast.635, ...), kind=kLoop, calls=%fused_computation.16 | loop fusion | flops 23068672 | bytes 16789504 | tf_op jit(solution)/shard_map/convert_element_type | solution.py:236
  124.2 2.1 fusion.33
  126.5 2.5 %collective-permute-start.11 = (f32[1,16,64,128]{3,2,1,0:T(8,128)}, f32[1,16,64,128]{3,2,1,0:T(8,128)}, u32[]{:S(2)}, u32[]{:S(2)}) collective-permute-start(f32[1,16,64,128]{3,2,1,0:T(8,128)} %bitcast.153), channel_id=1, source_target_pairs={{0,24},{8,0},{16,8},{24,16},{32,56},{40,32},{48,40},{56,48},{64,88... | collective-permute-start | bytes 1572872 | tf_op jit(solution)/shard_map/ppermute | solution.py:40
  129.4 1.6 fusion.19
  134.6 2.4 %multiply_reduce_fusion.10 = (f32[16]{0:T(128)}, f32[16]{0:T(128)}, f32[16]{0:T(128)}, f32[1,16,64,128]{3,2,1,0:T(8,128)S(1)}) fusion(f32[1,16,64,128]{3,2,1,0:T(8,128)S(1)} %copy-done.27, f32[8,16,64,128]{3,2,1,0:T(8,128)S(1)} %fusion.19, f32[16]{0:T(128)S(1)} %copy-done.56, f32[8,16,64,128]{3,2,1,0:T(8,128)} %copy-done.5, f32[16]{0:T(128)S(1)} %get-tuple-element.106, ...), kind=kLoop, calls=%fused_computation.172 | loop fusion | flops 1441744 | bytes 3670400 | tf_op jit(solution)/shard_map/transpose(jvp())/reduce_sum | solution.py:132
  137.1 2.3 fusion.24
  139.5 4.3 %fusion.72 = f32[8,128,1,128]{1,3,0,2:T(8,128)} fusion(f32[8,128,16,64]{1,0,3,2:T(8,128)S(1)} %copy-done.14, f32[1,1,16,64,128]{4,3,2,1,0:T(8,128)S(1)} %get-tuple-element.83, f32[1,1,16,64,128]{4,3,2,1,0:T(8,128)S(1)} %bitcast.614, f32[1,1,16,64,128]{4,3,2,1,0:T(8,128)S(1)} %bitcast.612, f32[1,1,16,64,128]{4,3,2,1,0:T(8,128)S(1)} %bitcast.610, ...), kind=kOutput, calls=%fused_computation.95 | convolution fusion | flops 811597824 | bytes 8388608 | tf_op jit(solution)/shard_map/transpose(jvp(kjgrp,kjgn->kgrpn))/dot_general | solution.py:126
  143.8 3.8 %fusion.21 = (f32[8,128,16]{1,2,0:T(8,128)S(1)}, f32[8,16,64,128]{3,2,1,0:T(8,128)}) fusion(f32[8,128,1,16,64]{1,0,4,3,2:T(8,128)S(1)} %bitcast.584, bf16[8,128,128,1]{2,1,3,0:T(8,128)(2,1)S(1)} %bitcast.589, f32[1,1,16,64,128]{4,3,2,1,0:T(8,128)S(1)} %get-tuple-element.83, f32[1,1,16,64,128]{4,3,2,1,0:T(8,128)S(1)} %bitcast.615, ...), kind=kOutput, calls=%fused_computation.33 | convolution fusion | flops 813678592 | bytes 12386304 | tf_op jit(solution)/shard_map/transpose(jvp(kjgrp,kjgn->kgrpn))/dot_general | solution.py:126
  150.5 12.5 %fusion.6 = (f32[8,16,128]{2,1,0:T(8,128)S(1)}, f32[8,16,128]{2,1,0:T(8,128)S(1)}, f32[8,128,128]{2,1,0:T(8,128)}) fusion(f32[8,128,128]{2,1,0:T(8,128)} %copy-done.40, f32[8,16,128]{2,1,0:T(8,128)S(1)} %bitcast.595, pred[128,128]{1,0:T(8,128)(4,1)} %copy-done.53, bf16[8,128,16,64]{1,0,3,2:T(8,128)(2,1)S(1)} %bitcast.602, f32[8,16,64,128]{3,0,2,1:T(8,128)} %bitcast.573), kind=kOutput, calls=%fused_computation.10 | convolution fusion | flops 824016896 | bytes 7553024 | tf_op jit(solution)/shard_map/transpose(jvp(kgrij,kjgrp->kigrp))/dot_general | solution.py:145
  163.1 7.4 %bitcast_add_fusion = f32[8,128,1,16,64]{1,4,3,0,2:T(8,128)} fusion(f32[8,16,64,128]{3,2,1,0:T(8,128)S(1)} %copy-done.88, f32[8,128,16]{1,2,0:T(8,128)S(1)} %copy-done.47, f32[8,128,128]{2,1,0:T(8,128)S(1)} %copy-done.41, f32[8,16,128]{2,1,0:T(8,128)S(1)} %bitcast.596, pred[128,128]{1,0:T(8,128)(4,1)S(1)} %copy-done.54, f32[8,16,64,128]{3,0,2,1:T(8,128)S(1)} %bitcast.574), kind=kOutput, calls=%fused_computation.22 | convolution fusion | flops 813694976 | bytes 13254656 | tf_op jit(solution)/shard_map/transpose(jvp(kgrij,kjgrp->kigrp))/dot_general | solution.py:145
  171.4 4.7 %fusion.77 = f32[8,128,1,128]{3,1,0,2:T(8,128)} fusion(f32[8,1,16,64,128]{4,3,2,1,0:T(8,128)S(1)} %copy-done.8, f32[8,128,1,16,64]{1,0,4,3,2:T(8,128)S(1)} %bitcast.575, f32[8,128,16]{1,2,0:T(8,128)S(1)} %copy-done.39), kind=kOutput, calls=%fused_computation.96 | convolution fusion | flops 806354944 | bytes 8978432 | tf_op jit(solution)/shard_map/transpose(jvp(kign,kgrpn->kigrp))/dot_general | solution.py:146
  176.0 4.1 %copy.118 = bf16[1024,1024]{1,0:T(8,128)(2,1)} copy(bf16[1024,1024]{0,1:T(8,128)(2,1)} %get-tuple-element.79) | data formatting | bytes 4194304
  180.1 2.5 %copy.120 = bf16[1024,1024]{1,0:T(8,128)(2,1)} copy(bf16[1024,1024]{0,1:T(8,128)(2,1)S(1)} %copy-done.15) | data formatting | bytes 4194304
  182.7 1.9 fusion.112
  184.7 1.2 collective-permute-start.12
  185.9 1.9 collective-permute-start.13
  187.8 1.1 collective-permute-start.14
  189.0 1.5 fusion.93
  190.5 4.3 %fusion.88 = f32[8,128,1,128]{3,1,0,2:T(8,128)} fusion(f32[8,128,1,128]{3,1,0,2:T(8,128)S(1)} %fusion.93, f32[8,128,1,16,64]{1,0,4,3,2:T(8,128)S(1)} %bitcast.576, f32[8,128,16]{1,2,0:T(8,128)S(1)} %copy-done.34, f32[1,16,64,128]{3,2,1,0:T(8,128)S(1)} %fusion.102), kind=kOutput, calls=%fused_computation.102 | convolution fusion | flops 806486016 | bytes 5832704 | tf_op jit(solution)/shard_map/transpose(jvp(kign,grpn->kigrp))/dot_general | solution.py:175
  194.8 1.8 collective-permute-done.12
  196.6 11.6 %collective-permute-done.13 = f32[1,16,64,128]{3,2,1,0:T(8,128)S(1)} collective-permute-done((f32[1,16,64,128]{3,2,1,0:T(8,128)S(1)}, f32[1,16,64,128]{3,2,1,0:T(8,128)S(1)}, u32[]{:S(2)}, u32[]{:S(2)}) %collective-permute-start.13) | collective-permute-done | bytes 524320 | tf_op jit(solution)/shard_map/ppermute | solution.py:40
  208.2 2.4 %collective-permute-done.14 = f32[1,16,64,128]{3,2,1,0:T(8,128)S(1)} collective-permute-done((f32[1,16,64,128]{3,2,1,0:T(8,128)S(1)}, f32[1,16,64,128]{3,2,1,0:T(8,128)S(1)}, u32[]{:S(2)}, u32[]{:S(2)}) %collective-permute-start.14) | collective-permute-done | bytes 524320 | tf_op jit(solution)/shard_map/ppermute | solution.py:40
  210.7 2.2 multiply_reduce_fusion.3
  212.9 1.4 fusion.82
  216.1 3.8 %fusion.16 = (f32[1024,16]{0,1:T(8,128)S(1)}, f32[1024,1,16,64]{0,3,2,1:T(8,128)S(1)}) fusion(f32[1024,1,16,64]{0,3,2,1:T(8,128)} %bitcast.577, f32[1024,16]{0,1:T(8,128)S(1)} %bitcast.618, bf16[1024,1,128]{2,0,1:T(8,128)(2,1)S(1)} %copy-done.17, f32[1,16,64,128]{3,2,1,0:T(8,128)S(1)} %get-tuple-element.57), kind=kOutput, calls=%fused_computation.26 | convolution fusion | flops 808435712 | bytes 9306112 | tf_op jit(solution)/shard_map/tgn,grpn->tgrp/dot_general | solution.py:159
  219.9 1.2 fusion.95
  221.9 1.0 copy.142
  222.9 1.2 copy-done.29
  224.1 1.1 fusion.32
  225.2 4.2 %copy.132 = bf16[8,128,1,16,64]{4,3,1,0,2:T(8,128)(2,1)} copy(bf16[8,128,1,16,64]{1,4,3,0,2:T(8,128)(2,1)S(1)} %fusion.32) | data formatting | bytes 4194304
  229.4 6.5 %reshape.1395 = bf16[1024,1024]{1,0:T(8,128)(2,1)} reshape(bf16[8,128,1,16,64]{4,3,1,0,2:T(8,128)(2,1)} %copy.132) | data formatting | bytes 4194304
  (265 shorter events, 32.3 us)
Async XLA Ops:
  0.6 40.4 %copy-start = (bf16[1024,1,128]{2,0,1:T(8,128)(2,1)S(1)}, bf16[1024,1,128]{2,0,1:T(8,128)(2,1)}, u32[]{:S(2)}) copy-start(bf16[1024,1,128]{2,0,1:T(8,128)(2,1)} %param.11) | copy-start | bytes 786436
  4.5 19.1 %copy-start.46 = (f32[8,128,16]{1,2,0:T(8,128)}, f32[8,128,16]{1,2,0:T(8,128)S(1)}, u32[]{:S(2)}) copy-start(f32[8,128,16]{1,2,0:T(8,128)S(1)} %get-tuple-element.94) | copy-start | bytes 196612
  4.5 38.9 %copy-start.38 = (f32[8,128,16]{1,2,0:T(8,128)}, f32[8,128,16]{1,2,0:T(8,128)S(1)}, u32[]{:S(2)}) copy-start(f32[8,128,16]{1,2,0:T(8,128)S(1)} %get-tuple-element.93) | copy-start | bytes 196612
  9.8 12.9 %copy-start.35 = (f32[1,16,8,128]{3,2,1,0:T(8,128)}, f32[1,16,8,128]{3,2,1,0:T(8,128)S(1)}, u32[]{:S(2)}) copy-start(f32[1,16,8,128]{3,2,1,0:T(8,128)S(1)} %broadcast_in_dim.281) | copy-start | bytes 196612
  10.9 52.6 %collective-permute-start = (f32[1,16,72,128]{3,2,1,0:T(8,128)}, f32[1,16,72,128]{3,2,1,0:T(8,128)}, u32[]{:S(2)}, u32[]{:S(2)}) collective-permute-start(f32[1,16,72,128]{3,2,1,0:T(8,128)} %get-tuple-element.89), channel_id=1, source_target_pairs={{0,8},{8,16},{16,24},{24,0},{32,40},{40,48},{48,56},{56,32},{64,72... | collective-permute-start | bytes 1769480 | tf_op jit(solution)/shard_map/ppermute | solution.py:40
  12.9 50.5 %collective-permute-start.1 = (f32[1,16,72,128]{3,2,1,0:T(8,128)}, f32[1,16,72,128]{3,2,1,0:T(8,128)}, u32[]{:S(2)}, u32[]{:S(2)}) collective-permute-start(f32[1,16,72,128]{3,2,1,0:T(8,128)} %get-tuple-element.89), channel_id=1, source_target_pairs={{0,16},{8,24},{16,0},{24,8},{32,48},{40,56},{48,32},{56,40},{64,80... | collective-permute-start | bytes 1769480 | tf_op jit(solution)/shard_map/ppermute | solution.py:40
  15.4 48.1 %collective-permute-start.2 = (f32[1,16,72,128]{3,2,1,0:T(8,128)}, f32[1,16,72,128]{3,2,1,0:T(8,128)}, u32[]{:S(2)}, u32[]{:S(2)}) collective-permute-start(f32[1,16,72,128]{3,2,1,0:T(8,128)} %get-tuple-element.89), channel_id=1, source_target_pairs={{0,24},{8,0},{16,8},{24,16},{32,56},{40,32},{48,40},{56,48},{64,88... | collective-permute-start | bytes 1769480 | tf_op jit(solution)/shard_map/ppermute | solution.py:40
  23.6 19.9 %copy-start.53 = (pred[128,128]{1,0:T(8,128)(4,1)}, pred[128,128]{1,0:T(8,128)(4,1)S(1)}, u32[]{:S(2)}) copy-start(pred[128,128]{1,0:T(8,128)(4,1)S(1)} %iota_compare_fusion.6) | copy-start | bytes 49156
  28.8 9.9 %copy-start.55 = (f32[16]{0:T(128)}, f32[16]{0:T(128)S(1)}, u32[]{:S(2)}) copy-start(f32[16]{0:T(128)S(1)} %get-tuple-element.105) | copy-start | bytes 196
  28.8 10.1 %copy-start.69 = (f32[16]{0:T(128)}, f32[16]{0:T(128)S(1)}, u32[]{:S(2)}) copy-start(f32[16]{0:T(128)S(1)} %get-tuple-element.104) | copy-start | bytes 196
  28.9 10.9 %copy-start.61 = (f32[16]{0:T(128)}, f32[16]{0:T(128)S(1)}, u32[]{:S(2)}) copy-start(f32[16]{0:T(128)S(1)} %get-tuple-element.103) | copy-start | bytes 196
  28.9 11.0 %copy-start.63 = (f32[16]{0:T(128)}, f32[16]{0:T(128)S(1)}, u32[]{:S(2)}) copy-start(f32[16]{0:T(128)S(1)} %get-tuple-element.102) | copy-start | bytes 196
  28.9 11.2 %copy-start.65 = (f32[16]{0:T(128)}, f32[16]{0:T(128)S(1)}, u32[]{:S(2)}) copy-start(f32[16]{0:T(128)S(1)} %get-tuple-element.101) | copy-start | bytes 196
  28.9 11.3 %copy-start.67 = (f32[16]{0:T(128)}, f32[16]{0:T(128)S(1)}, u32[]{:S(2)}) copy-start(f32[16]{0:T(128)S(1)} %get-tuple-element.100) | copy-start | bytes 196
  33.4 5.2 %copy-start.6 = (f32[8,1,16,64,128]{4,3,2,1,0:T(8,128)S(1)}, f32[8,1,16,64,128]{4,3,2,1,0:T(8,128)}, u32[]{:S(2)}) copy-start(f32[8,1,16,64,128]{4,3,2,1,0:T(8,128)} %broadcast_dynamic-update-slice_fusion) | copy-start | bytes 12582916
  43.1 8.8 %copy-start.10 = (f32[8,16,64,128]{3,2,1,0:T(8,128)}, f32[8,16,64,128]{3,2,1,0:T(8,128)S(1)}, u32[]{:S(2)}) copy-start(f32[8,16,64,128]{3,2,1,0:T(8,128)S(1)} %fusion.30) | copy-start | bytes 12582916
  43.4 8.5 %copy-start.40 = (f32[8,128,128]{2,1,0:T(8,128)}, f32[8,128,128]{2,1,0:T(8,128)S(1)}, u32[]{:S(2)}) copy-start(f32[8,128,128]{2,1,0:T(8,128)S(1)} %fusion.168) | copy-start | bytes 1572868
  52.5 9.7 %copy-start.81 = (pred[4]{0:T(512)(128)(4,1)S(1)}, pred[4]{0:T(512)(128)(4,1)}, u32[]{:S(2)}) copy-start(pred[4]{0:T(512)(128)(4,1)} %get-tuple-element.143) | copy-start | bytes 16
  52.5 11.0 %copy-start.30 = (f32[1,1,16,72,128]{4,3,2,1,0:T(8,128)S(1)}, f32[1,1,16,72,128]{4,3,2,1,0:T(8,128)}, u32[]{:S(2)}) copy-start(f32[1,1,16,72,128]{4,3,2,1,0:T(8,128)} %get-tuple-element.88) | copy-start | bytes 1769476
  64.6 33.3 %copy-start.79 = (pred[4,4]{1,0:T(4,128)(4,1)S(1)}, pred[4,4]{1,0:T(4,128)(4,1)}, u32[]{:S(2)}) copy-start(pred[4,4]{1,0:T(4,128)(4,1)} %get-tuple-element.133) | copy-start | bytes 52
  64.6 33.3 %copy-start.80 = (pred[4,4]{1,0:T(4,128)(4,1)S(1)}, pred[4,4]{1,0:T(4,128)(4,1)}, u32[]{:S(2)}) copy-start(pred[4,4]{1,0:T(4,128)(4,1)} %get-tuple-element.134) | copy-start | bytes 52
  64.6 33.4 %copy-start.85 = (pred[4]{0:T(512)(128)(4,1)S(1)}, pred[4]{0:T(512)(128)(4,1)}, u32[]{:S(2)}) copy-start(pred[4]{0:T(512)(128)(4,1)} %copy-done.84) | copy-start | bytes 16
  67.7 32.2 %copy-start.28 = (f32[8,128,1,16,64]{1,4,3,0,2:T(8,128)S(1)}, f32[8,128,1,16,64]{1,4,3,0,2:T(8,128)}, u32[]{:S(2)}) copy-start(f32[8,128,1,16,64]{1,4,3,0,2:T(8,128)} %bitcast_add_fusion.1) | copy-start | bytes 12582916
  67.7 32.2 %copy-start.34 = (f32[8,128,16]{1,2,0:T(8,128)S(1)}, f32[8,128,16]{1,2,0:T(8,128)}, u32[]{:S(2)}) copy-start(f32[8,128,16]{1,2,0:T(8,128)} %get-tuple-element.92) | copy-start | bytes 196612
  67.8 16.0 %collective-permute-start.3 = (f32[1,16,72,128]{3,2,1,0:T(8,128)S(1)}, f32[1,16,72,128]{3,2,1,0:T(8,128)S(1)}, u32[]{:S(2)}, u32[]{:S(2)}) collective-permute-start(f32[1,16,72,128]{3,2,1,0:T(8,128)S(1)} %get-tuple-element.87), channel_id=1, source_target_pairs={{0,32},{32,64},{64,96},{96,0},{8,40},{40,72},{72,104},{104,8},{16,... | collective-permute-start | bytes 1769480 | tf_op jit(solution)/shard_map/ppermute | solution.py:40
  69.5 27.8 %collective-permute-start.4 = (f32[1,16,72,128]{3,2,1,0:T(8,128)S(1)}, f32[1,16,72,128]{3,2,1,0:T(8,128)S(1)}, u32[]{:S(2)}, u32[]{:S(2)}) collective-permute-start(f32[1,16,72,128]{3,2,1,0:T(8,128)S(1)} %get-tuple-element.87), channel_id=1, source_target_pairs={{0,64},{32,96},{64,0},{96,32},{8,72},{40,104},{72,8},{104,40},{16,... | collective-permute-start | bytes 1769480 | tf_op jit(solution)/shard_map/ppermute | solution.py:40
  72.8 24.9 %collective-permute-start.5 = (f32[1,16,72,128]{3,2,1,0:T(8,128)S(1)}, f32[1,16,72,128]{3,2,1,0:T(8,128)S(1)}, u32[]{:S(2)}, u32[]{:S(2)}) collective-permute-start(f32[1,16,72,128]{3,2,1,0:T(8,128)S(1)} %get-tuple-element.87), channel_id=1, source_target_pairs={{0,96},{32,0},{64,32},{96,64},{8,104},{40,8},{72,40},{104,72},{16,... | collective-permute-start | bytes 1769480 | tf_op jit(solution)/shard_map/ppermute | solution.py:40
  104.8 7.5 %copy-start.83 = (pred[4]{0:T(512)(128)(4,1)S(1)}, pred[4]{0:T(512)(128)(4,1)}, u32[]{:S(2)}) copy-start(pred[4]{0:T(512)(128)(4,1)} %copy-done.82) | copy-start | bytes 16
  107.7 3.2 %collective-permute-start.6 = (f32[2,1024]{1,0:T(2,128)S(1)}, f32[2,1024]{1,0:T(2,128)S(1)}, u32[]{:S(2)}, u32[]{:S(2)}) collective-permute-start(f32[2,1024]{1,0:T(2,128)S(1)} %pad_maximum_fusion.8), channel_id=1, source_target_pairs={{0,1},{1,0},{2,3},{3,2},{4,5},{5,4},{6,7},{7,6},{8,9},{9,8},{10,11... | collective-permute-start | bytes 24584 | tf_op jit(solution)/shard_map/ppermute | solution.py:96
  111.0 2.6 %collective-permute-start.7 = (f32[2,1024]{1,0:T(2,128)S(1)}, f32[2,1024]{1,0:T(2,128)S(1)}, u32[]{:S(2)}, u32[]{:S(2)}) collective-permute-start(f32[2,1024]{1,0:T(2,128)S(1)} %fusion.161), channel_id=1, source_target_pairs={{0,2},{1,3},{2,0},{3,1},{4,6},{5,7},{6,4},{7,5},{8,10},{9,11},{10,... | collective-permute-start | bytes 24584 | tf_op jit(solution)/shard_map/ppermute | solution.py:96
  113.6 4.1 %collective-permute-start.8 = (f32[2,1024]{1,0:T(2,128)S(1)}, f32[2,1024]{1,0:T(2,128)S(1)}, u32[]{:S(2)}, u32[]{:S(2)}) collective-permute-start(f32[2,1024]{1,0:T(2,128)S(1)} %fusion.181), channel_id=1, source_target_pairs={{0,4},{1,5},{2,6},{3,7},{4,0},{5,1},{6,2},{7,3},{8,12},{9,13},{10,... | collective-permute-start | bytes 24584 | tf_op jit(solution)/shard_map/ppermute | solution.py:96
  123.7 13.4 %copy-start.1 = (f32[128,8,8,128]{3,2,1,0:T(8,128)}, f32[128,8,8,128]{3,2,1,0:T(8,128)S(1)}, u32[]{:S(2)}) copy-start(f32[128,8,8,128]{3,2,1,0:T(8,128)S(1)} %copy.139) | copy-start | bytes 12582916
  124.2 5.2 %copy-start.39 = (f32[8,128,16]{1,2,0:T(8,128)S(1)}, f32[8,128,16]{1,2,0:T(8,128)}, u32[]{:S(2)}) copy-start(f32[8,128,16]{1,2,0:T(8,128)} %copy-done.38) | copy-start | bytes 196612
  126.2 56.4 %collective-permute-start.10 = (f32[1,16,64,128]{3,2,1,0:T(8,128)}, f32[1,16,64,128]{3,2,1,0:T(8,128)}, u32[]{:S(2)}, u32[]{:S(2)}) collective-permute-start(f32[1,16,64,128]{3,2,1,0:T(8,128)} %bitcast.153), channel_id=1, source_target_pairs={{0,16},{8,24},{16,0},{24,8},{32,48},{40,56},{48,32},{56,40},{64,80... | collective-permute-start | bytes 1572872 | tf_op jit(solution)/shard_map/ppermute | solution.py:40
  126.5 56.2 %collective-permute-start.11 = (f32[1,16,64,128]{3,2,1,0:T(8,128)}, f32[1,16,64,128]{3,2,1,0:T(8,128)}, u32[]{:S(2)}, u32[]{:S(2)}) collective-permute-start(f32[1,16,64,128]{3,2,1,0:T(8,128)} %bitcast.153), channel_id=1, source_target_pairs={{0,24},{8,0},{16,8},{24,16},{32,56},{40,32},{48,40},{56,48},{64,88... | collective-permute-start | bytes 1572872 | tf_op jit(solution)/shard_map/ppermute | solution.py:40
  129.0 53.7 %collective-permute-start.9 = (f32[1,16,64,128]{3,2,1,0:T(8,128)}, f32[1,16,64,128]{3,2,1,0:T(8,128)}, u32[]{:S(2)}, u32[]{:S(2)}) collective-permute-start(f32[1,16,64,128]{3,2,1,0:T(8,128)} %bitcast.153), channel_id=1, source_target_pairs={{0,8},{8,16},{16,24},{24,0},{32,40},{40,48},{48,56},{56,32},{64,72... | collective-permute-start | bytes 1572872 | tf_op jit(solution)/shard_map/ppermute | solution.py:40
  143.8 6.7 %copy-start.32 = (bf16[128,8,8,128]{3,2,1,0:T(8,128)(2,1)S(1)}, bf16[128,8,8,128]{3,2,1,0:T(8,128)(2,1)}, u32[]{:S(2)}) copy-start(bf16[128,8,8,128]{3,2,1,0:T(8,128)(2,1)} %copy.136) | copy-start | bytes 6291460
  150.5 12.6 %copy-start.2 = (f32[128,8,8,128]{3,2,1,0:T(8,128)S(1)}, f32[128,8,8,128]{3,2,1,0:T(8,128)}, u32[]{:S(2)}) copy-start(f32[128,8,8,128]{3,2,1,0:T(8,128)} %copy-done.1) | copy-start | bytes 12582916
  150.5 12.6 %copy-start.41 = (f32[8,128,128]{2,1,0:T(8,128)S(1)}, f32[8,128,128]{2,1,0:T(8,128)}, u32[]{:S(2)}) copy-start(f32[8,128,128]{2,1,0:T(8,128)} %copy-done.40) | copy-start | bytes 1572868
  150.5 12.6 %copy-start.47 = (f32[8,128,16]{1,2,0:T(8,128)S(1)}, f32[8,128,16]{1,2,0:T(8,128)}, u32[]{:S(2)}) copy-start(f32[8,128,16]{1,2,0:T(8,128)} %copy-done.46) | copy-start | bytes 196612
  150.5 12.5 %copy-start.54 = (pred[128,128]{1,0:T(8,128)(4,1)S(1)}, pred[128,128]{1,0:T(8,128)(4,1)}, u32[]{:S(2)}) copy-start(pred[128,128]{1,0:T(8,128)(4,1)} %copy-done.53) | copy-start | bytes 49156
  150.5 12.5 %copy-start.88 = (f32[8,16,64,128]{3,2,1,0:T(8,128)S(1)}, f32[8,16,64,128]{3,2,1,0:T(8,128)}, u32[]{:S(2)}) copy-start(f32[8,16,64,128]{3,2,1,0:T(8,128)} %get-tuple-element.142) | copy-start | bytes 12582916
  163.0 7.4 %copy-start.50 = (f32[8,128,16]{1,2,0:T(8,128)S(1)}, f32[8,128,16]{1,2,0:T(8,128)}, u32[]{:S(2)}) copy-start(f32[8,128,16]{1,2,0:T(8,128)} %copy-done.49) | copy-start | bytes 196612
  163.0 7.4 %copy-start.51 = (f32[8,1,16,1]{3,2,0,1:T(8,128)S(1)}, f32[8,1,16,1]{3,2,0,1:T(8,128)}, u32[]{:S(2)}) copy-start(f32[8,1,16,1]{3,2,0,1:T(8,128)} %copy.104) | copy-start | bytes 1540
  163.1 8.3 %copy-start.8 = (f32[8,1,16,64,128]{4,3,2,1,0:T(8,128)S(1)}, f32[8,1,16,64,128]{4,3,2,1,0:T(8,128)}, u32[]{:S(2)}) copy-start(f32[8,1,16,64,128]{4,3,2,1,0:T(8,128)} %copy-done.7) | copy-start | bytes 12582916
  176.0 6.7 %copy-start.57 = (f32[16]{0:T(128)S(1)}, f32[16]{0:T(128)}, u32[]{:S(2)}) copy-start(f32[16]{0:T(128)} %get-tuple-element.115) | copy-start | bytes 196
  176.0 6.7 %copy-start.58 = (f32[16]{0:T(128)S(1)}, f32[16]{0:T(128)}, u32[]{:S(2)}) copy-start(f32[16]{0:T(128)} %get-tuple-element.116) | copy-start | bytes 196
  176.0 6.7 %copy-start.59 = (f32[16]{0:T(128)S(1)}, f32[16]{0:T(128)}, u32[]{:S(2)}) copy-start(f32[16]{0:T(128)} %get-tuple-element.117) | copy-start | bytes 196
  176.0 6.7 %copy-start.60 = (f32[16]{0:T(128)S(1)}, f32[16]{0:T(128)}, u32[]{:S(2)}) copy-start(f32[16]{0:T(128)} %get-tuple-element.118) | copy-start | bytes 196
  182.7 7.8 %copy-start.3 = (f32[128,8,8,128]{3,2,1,0:T(8,128)S(1)}, f32[128,8,8,128]{3,2,1,0:T(8,128)}, u32[]{:S(2)}) copy-start(f32[128,8,8,128]{3,2,1,0:T(8,128)} %copy-done.1) | copy-start | bytes 12582916
  184.6 26.0 %copy-start.71 = (f32[16]{0:T(128)S(1)}, f32[16]{0:T(128)}, u32[]{:S(2)}) copy-start(f32[16]{0:T(128)} %get-tuple-element.107) | copy-start | bytes 196
  184.6 26.0 %copy-start.72 = (f32[16]{0:T(128)S(1)}, f32[16]{0:T(128)}, u32[]{:S(2)}) copy-start(f32[16]{0:T(128)} %get-tuple-element.108) | copy-start | bytes 196
  184.6 26.0 %copy-start.73 = (f32[16]{0:T(128)S(1)}, f32[16]{0:T(128)}, u32[]{:S(2)}) copy-start(f32[16]{0:T(128)} %get-tuple-element.109) | copy-start | bytes 196
  184.6 26.0 %copy-start.74 = (f32[16]{0:T(128)S(1)}, f32[16]{0:T(128)}, u32[]{:S(2)}) copy-start(f32[16]{0:T(128)} %get-tuple-element.110) | copy-start | bytes 196
  184.6 26.0 %copy-start.75 = (f32[16]{0:T(128)S(1)}, f32[16]{0:T(128)}, u32[]{:S(2)}) copy-start(f32[16]{0:T(128)} %get-tuple-element.111) | copy-start | bytes 196
  184.6 26.0 %copy-start.76 = (f32[16]{0:T(128)S(1)}, f32[16]{0:T(128)}, u32[]{:S(2)}) copy-start(f32[16]{0:T(128)} %get-tuple-element.112) | copy-start | bytes 196
  184.7 26.0 %copy-start.77 = (f32[16]{0:T(128)S(1)}, f32[16]{0:T(128)}, u32[]{:S(2)}) copy-start(f32[16]{0:T(128)} %get-tuple-element.113) | copy-start | bytes 196
  184.7 26.0 %copy-start.78 = (f32[16]{0:T(128)S(1)}, f32[16]{0:T(128)}, u32[]{:S(2)}) copy-start(f32[16]{0:T(128)} %get-tuple-element.114) | copy-start | bytes 196
  184.7 26.0 %copy-start.87 = (f32[16]{0:T(128)S(1)}, f32[16]{0:T(128)}, u32[]{:S(2)}) copy-start(f32[16]{0:T(128)} %exp.181) | copy-start | bytes 196
  184.7 11.9 %collective-permute-start.12 = (f32[1,16,64,128]{3,2,1,0:T(8,128)S(1)}, f32[1,16,64,128]{3,2,1,0:T(8,128)S(1)}, u32[]{:S(2)}, u32[]{:S(2)}) collective-permute-start(f32[1,16,64,128]{3,2,1,0:T(8,128)S(1)} %fusion.112), channel_id=1, source_target_pairs={{0,32},{32,64},{64,96},{96,0},{8,40},{40,72},{72,104},{104,8},{16,... | collective-permute-start | bytes 1572872 | tf_op jit(solution)/shard_map/ppermute | solution.py:40
  185.9 22.3 %collective-permute-start.13 = (f32[1,16,64,128]{3,2,1,0:T(8,128)S(1)}, f32[1,16,64,128]{3,2,1,0:T(8,128)S(1)}, u32[]{:S(2)}, u32[]{:S(2)}) collective-permute-start(f32[1,16,64,128]{3,2,1,0:T(8,128)S(1)} %fusion.112), channel_id=1, source_target_pairs={{0,64},{32,96},{64,0},{96,32},{8,72},{40,104},{72,8},{104,40},{16,... | collective-permute-start | bytes 1572872 | tf_op jit(solution)/shard_map/ppermute | solution.py:40
  187.8 22.8 %collective-permute-start.14 = (f32[1,16,64,128]{3,2,1,0:T(8,128)S(1)}, f32[1,16,64,128]{3,2,1,0:T(8,128)S(1)}, u32[]{:S(2)}, u32[]{:S(2)}) collective-permute-start(f32[1,16,64,128]{3,2,1,0:T(8,128)S(1)} %fusion.112), channel_id=1, source_target_pairs={{0,96},{32,0},{64,32},{96,64},{8,104},{40,8},{72,40},{104,72},{16,... | collective-permute-start | bytes 1572872 | tf_op jit(solution)/shard_map/ppermute | solution.py:40
  190.5 22.4 %copy-start.4 = (f32[1024,1024]{0,1:T(8,128)S(1)}, f32[1024,1024]{0,1:T(8,128)}, u32[]{:S(2)}) copy-start(f32[1024,1024]{0,1:T(8,128)} %get-tuple-element.84) | copy-start | bytes 12582916
  190.5 22.4 %copy-start.37 = (f32[2,8,8,128]{3,1,2,0:T(8,128)S(1)}, f32[2,8,8,128]{3,1,2,0:T(8,128)}, u32[]{:S(2)}) copy-start(f32[2,8,8,128]{3,1,2,0:T(8,128)} %copy-done.36) | copy-start | bytes 196612
  (40 other events, 105.2 us)
where the time goes:
time: 240 us; the launch traced here: 236 us
  matrix products  63.9 us (27%)
  local copies, waits for them, and re-layouts  56.3 us (23%)
  other arithmetic  48.6 us (20%)
  waiting for transfers between devices  39.4 us (16%)
  starting transfers between devices  25.6 us (11%)
    unnamed x193, local copies, waits for them, and re-layouts  45.9 us
    ppermute x12, waiting for transfers between devices, grouped_gather(): parts.append(lax.ppermute(value, 'seq', pairs))  37.7 us
    dot_general x3, matrix products, local_core(): jnp.einsum('kgrij,kjgrp->kigrp', weighted, x_blocks, precision=PRECISION)  27.7 us
    ppermute x12, starting transfers between devices, grouped_gather(): parts.append(lax.ppermute(value, 'seq', pairs))  19.1 us
    dot_general x3, matrix products, block_chain(): jnp.einsum('kjgrp,kjgn->kgrpn', scaled, b_blocks, precision=PRECISION)  9.66 us
    dot_general x3, matrix products, local_core(): jnp.einsum('kign,kgrpn->kigrp', c_blocks, starts, precision=PRECISION)  7.66 us
    ppermute x3, starting transfers between devices, head_sum(): values = values + lax.ppermute(values, 'head', pairs)  6.5 us
    dot_general x2, matrix products, add_incoming(): jnp.einsum('kign,grpn->kigrp', c_blocks, incoming, precision=PRECISION)  5.88 us
  transfers between devices with their start and end apart: 15, of which 8 were waited for; matrix products, arithmetic and copies ran while one was open for 43% of the time, Pallas kernels for 0%

commit v1 on v0

--- a/solution.py
+++ b/solution.py
@@ -236,8 +236,11 @@
     ).astype(jnp.bfloat16)
     grad_ssd = grad_gated * gate_silu
     upstream = grad_ssd.reshape(blocks, SPAN, groups, per_group, head_size)
-    reached = upstream * jnp.moveaxis(reach, 3, 1)[..., None]
-    leaving = jnp.einsum("kign,kigrp->grpn", c_blocks, reached, precision=PRECISION)
+    reach_tok = jnp.moveaxis(reach, 3, 1).reshape(tok_rows, groups, per_group)
+    reached = grad_ssd.reshape(tok_rows, groups, per_group, head_size) * reach_tok[..., None]
+    leaving = jnp.einsum(
+        "tgrp,tgn->grpn", reached, c_matrix.astype(jnp.float32), precision=PRECISION
+    )
     adjoint = suffix_state(leaving, seq_logs)
     light_grads = light_pull(upstream)
     core_grads = lax.optimization_barrier(core_pull(tuple(light_grads[:2])))

time: 240 us -> 239 us (level)
  local copies, waits for them, and re-layouts: 56.3 us -> 53.7 us
    convert_element_type x1 -> x0, other arithmetic: 5.03 us -> none  [device_body(): grad_gate = (grad_gated * ssd_out * sigmoid_gate * (1.0 + gate_value * (1...]
    dot_general x3, matrix products: 7.66 us -> 12.2 us  [local_core(): jnp.einsum('kign,kgrpn->kigrp', c_blocks, starts, precision=PRECISION)]
    mul x2 -> x1, other arithmetic: 1.13 us -> 5.39 us  [device_body(): grad_ssd.reshape(tok_rows, groups, per_group, head_size)]
    convert_element_type x1, other arithmetic: 1.07 us -> 4.53 us  [device_body(): grad_inputs = grad_x.reshape(tok_rows, width).astype(jnp.bfloat16)]
    unnamed x193 -> x202, local copies, waits for them, and re-layouts: 45.9 us -> 45.4 us
  transfers between devices with their start and end apart: 15 -> 15, of which waited for: 8 -> 6; matrix products, arithmetic and copies ran while one was open for 43% -> 41% of each run, Pallas kernels for 0% -> 0%
where the time goes in v1:
time: 239 us; the launch traced here: 235 us
  matrix products  62.5 us (26%)
  local copies, waits for them, and re-layouts  53.7 us (22%)
  other arithmetic  50.4 us (21%)
  waiting for transfers between devices  41.3 us (17%)
  starting transfers between devices  24.9 us (10%)
    unnamed x202, local copies, waits for them, and re-layouts  45.4 us
    ppermute x12, waiting for transfers between devices, grouped_gather(): parts.append(lax.ppermute(value, 'seq', pairs))  39.7 us
    dot_general x3, matrix products, local_core(): jnp.einsum('kgrij,kjgrp->kigrp', weighted, x_blocks, precision=PRECISION)  27.2 us
    ppermute x12, starting transfers between devices, grouped_gather(): parts.append(lax.ppermute(value, 'seq', pairs))  19.2 us
    dot_general x3, matrix products, local_core(): jnp.einsum('kign,kgrpn->kigrp', c_blocks, starts, precision=PRECISION)  12.2 us
    dot_general x3, matrix products, block_chain(): jnp.einsum('kjgrp,kjgn->kgrpn', scaled, b_blocks, precision=PRECISION)  8.22 us
    reduce_sum x5, other arithmetic, block_chain(): carried = factors[block][..., None, None] * carried + block_states[block]  7.98 us
    dot_general x2, matrix products, add_incoming(): jnp.einsum('kign,grpn->kigrp', c_blocks, incoming, precision=PRECISION)  5.77 us
  transfers between devices with their start and end apart: 15, of which 6 were waited for; matrix products, arithmetic and copies ran while one was open for 41% of the time, Pallas kernels for 0%

profile of v1, /device:TPU:1, one launch (start us, length us, event | category | flops | bytes accessed | tf_op | source)
XLA Modules:
  0.0 235.1 jit_solution(12788889858604542096)
XLA Ops:
  2.7 1.0 reduce_sum.266
  5.1 2.9 %copy.78 = bf16[1024,1024]{0,1:T(8,128)(2,1)S(1)} copy(bf16[1024,1024]{1,0:T(8,128)(2,1)} %param.7) | data formatting | bytes 4194304 | tf_op args[0]
  9.0 1.3 convolution_bitcast_fusion.2
  10.3 1.1 fusion.165
  11.4 3.6 %collective-permute-start.1 = (f32[1,16,72,128]{3,2,1,0:T(8,128)}, f32[1,16,72,128]{3,2,1,0:T(8,128)}, u32[]{:S(2)}, u32[]{:S(2)}) collective-permute-start(f32[1,16,72,128]{3,2,1,0:T(8,128)} %get-tuple-element.90), channel_id=1, source_target_pairs={{0,16},{8,24},{16,0},{24,8},{32,48},{40,56},{48,32},{56,40},{64,80... | collective-permute-start | bytes 1769480 | tf_op jit(solution)/shard_map/ppermute | solution.py:40
  15.3 2.5 %collective-permute-start.2 = (f32[1,16,72,128]{3,2,1,0:T(8,128)}, f32[1,16,72,128]{3,2,1,0:T(8,128)}, u32[]{:S(2)}, u32[]{:S(2)}) collective-permute-start(f32[1,16,72,128]{3,2,1,0:T(8,128)} %get-tuple-element.90), channel_id=1, source_target_pairs={{0,24},{8,0},{16,8},{24,16},{32,56},{40,32},{48,40},{56,48},{64,88... | collective-permute-start | bytes 1769480 | tf_op jit(solution)/shard_map/ppermute | solution.py:40
  19.8 4.4 %fusion.168 = (f32[1024,1024]{0,1:T(8,128)}, f32[128,8,8,128]{3,1,2,0:T(8,128)}) fusion(bf16[1024,1024]{0,1:T(8,128)(2,1)S(1)} %copy.78), kind=kLoop, calls=%fused_computation.310 | loop fusion | flops 1048576 | bytes 10485760 | tf_op jit(solution)/shard_map/convert_element_type | solution.py:188
  26.4 1.0 copy.133
  28.1 1.3 copy-done.12
  29.4 1.6 fusion.51
  31.4 3.1 %copy-done.7 = f32[8,1,16,64,128]{4,3,2,1,0:T(8,128)S(1)} copy-done((f32[8,1,16,64,128]{4,3,2,1,0:T(8,128)S(1)}, f32[8,1,16,64,128]{4,3,2,1,0:T(8,128)}, u32[]{:S(2)}) %copy-start.7) | copy-done | bytes 4194328
  36.9 1.4 fusion.30
  38.9 8.2 %bitcast_add_fusion.1 = f32[8,128,1,16,64]{1,4,3,0,2:T(8,128)} fusion(f32[8,16,64,128]{3,2,1,0:T(8,128)S(1)} %fusion.30, f32[8,128,16]{1,2,0:T(8,128)S(1)} %get-tuple-element.95, f32[8,128,128]{2,1,0:T(8,128)S(1)} %fusion.171, f32[8,16,128]{2,1,0:T(8,128)S(1)} %bitcast.593, pred[128,128]{1,0:T(8,128)(4,1)S(1)} %iota_compare_fusion.6, ...), kind=kOutput, calls=%fused_computation.23 | convolution fusion | flops 813694976 | bytes 11157504 | tf_op jit(solution)/shard_map/jvp(kgrij,kjgrp->kigrp)/dot_general | solution.py:145
  48.4 2.9 %copy.86 = bf16[1024,1024]{0,1:T(8,128)(2,1)S(1)} copy(bf16[1024,1024]{1,0:T(8,128)(2,1)} %param.8) | data formatting | bytes 4194304 | tf_op args[1]
  51.3 3.9 %copy.87 = bf16[1024,1024]{0,1:T(8,128)(2,1)} copy(bf16[1024,1024]{1,0:T(8,128)(2,1)} %param.13) | data formatting | bytes 4194304 | tf_op args[6]
  55.3 1.4 compare_and_fusion.5
  56.7 1.4 compare_and_fusion.3
  58.1 1.1 fusion.119
  60.7 1.6 multiply_add_fusion
  62.5 3.7 %collective-permute-start.4 = (f32[1,16,72,128]{3,2,1,0:T(8,128)S(1)}, f32[1,16,72,128]{3,2,1,0:T(8,128)S(1)}, u32[]{:S(2)}, u32[]{:S(2)}) collective-permute-start(f32[1,16,72,128]{3,2,1,0:T(8,128)S(1)} %get-tuple-element.88), channel_id=1, source_target_pairs={{0,64},{32,96},{64,0},{96,32},{8,72},{40,104},{72,8},{104,40},{16,... | collective-permute-start | bytes 1769480 | tf_op jit(solution)/shard_map/ppermute | solution.py:40
  66.9 2.1 collective-permute-start.5
  70.4 8.0 %collective-permute-done.4 = f32[1,16,72,128]{3,2,1,0:T(8,128)S(1)} collective-permute-done((f32[1,16,72,128]{3,2,1,0:T(8,128)S(1)}, f32[1,16,72,128]{3,2,1,0:T(8,128)S(1)}, u32[]{:S(2)}, u32[]{:S(2)}) %collective-permute-start.4) | collective-permute-done | bytes 589856 | tf_op jit(solution)/shard_map/ppermute | solution.py:40
  78.4 14.2 %collective-permute-done.3 = f32[1,16,72,128]{3,2,1,0:T(8,128)S(1)} collective-permute-done((f32[1,16,72,128]{3,2,1,0:T(8,128)S(1)}, f32[1,16,72,128]{3,2,1,0:T(8,128)S(1)}, u32[]{:S(2)}, u32[]{:S(2)}) %collective-permute-start.3) | collective-permute-done | bytes 589856 | tf_op jit(solution)/shard_map/ppermute | solution.py:40
  93.0 1.7 fusion.101
  94.8 1.5 fusion.23
  96.3 3.3 %copy.85 = f32[8,128,1,16,64]{1,0,4,3,2:T(8,128)S(1)} copy(f32[8,128,1,16,64]{1,4,3,0,2:T(8,128)S(1)} %get-tuple-element.141) | data formatting | bytes 8388608 | tf_op jit(solution)/shard_map/jvp()/add | solution.py:176
  99.6 2.9 %multiply_reduce_fusion.2 = (f32[1024]{0:T(1024)S(1)}, f32[1024]{0:T(1024)S(1)}) fusion(bf16[1024,1024]{0,1:T(8,128)(2,1)S(1)} %copy.86, f32[128,8,8,128]{3,2,1,0:T(8,128)S(1)} %bitcast.577, bf16[1024,1024]{0,1:T(8,128)(2,1)S(1)} %copy-done.9, f32[1024]{0:T(1024)S(1)} %copy-done.57), kind=kLoop, calls=%fused_computation.61 | loop fusion | flops 12580864 | bytes 8400896 | tf_op jit(solution)/shard_map/reduce_sum | solution.py:226
  102.5 1.3 collective-permute-start.6
  105.0 1.4 collective-permute-start.7
  106.5 1.1 collective-permute-done.7
  107.6 3.0 %collective-permute-start.8 = (f32[2,1024]{1,0:T(2,128)S(1)}, f32[2,1024]{1,0:T(2,128)S(1)}, u32[]{:S(2)}, u32[]{:S(2)}) collective-permute-start(f32[2,1024]{1,0:T(2,128)S(1)} %fusion.184), channel_id=1, source_target_pairs={{0,4},{1,5},{2,6},{3,7},{4,0},{5,1},{6,2},{7,3},{8,12},{9,13},{10,... | collective-permute-start | bytes 24584 | tf_op jit(solution)/shard_map/ppermute | solution.py:96
  111.8 5.4 %bitcast_multiply_fusion.4 = (f32[1024,1024]{0,1:T(8,128)S(1)}, f32[1024,1024]{0,1:T(8,128)S(1)}, bf16[1024,1024]{0,1:T(8,128)(2,1)}, bf16[1024,1024]{0,1:T(8,128)(2,1)}) fusion(f32[1024,16]{0,1:T(8,128)S(1)} %bitcast.621, f32[1024]{0:T(1024)S(1)} %fusion.150, bf16[1024,1024]{0,1:T(8,128)(2,1)S(1)} %copy.86, f32[128,8,8,128]{3,2,1,0:T(8,128)S(1)} %bitcast.578, ...), kind=kLoop, calls=%fused_computation.27 | loop fusion | flops 24117248 | bytes 21049344 | tf_op jit(solution)/shard_map/mul | solution.py:240
  117.2 2.1 fusion.120
  121.0 1.0 copy.135
  122.0 3.6 %fusion.19 = f32[8,16,64,128]{3,2,1,0:T(8,128)} fusion(bf16[8,128,128,1]{2,1,3,0:T(8,128)(2,1)S(1)} %bitcast.566, f32[8,128,1,16,64]{1,0,4,3,2:T(8,128)S(1)} %bitcast.569, f32[8,128,16]{1,2,0:T(8,128)S(1)} %copy-done.40), kind=kOutput, calls=%fused_computation.30 | convolution fusion | flops 806354944 | bytes 8716288 | tf_op jit(solution)/shard_map/transpose(jvp(kign,kgrpn->kigrp))/dot_general | solution.py:146
  125.6 1.4 copy-done.11
  127.1 2.9 %fusion.24 = (f32[8,128,16]{1,2,0:T(8,128)}, f32[8,128,16]{1,2,0:T(8,128)}) fusion(f32[16,64,8,128]{3,1,0,2:T(8,128)S(1)} %get-tuple-element.142, f32[8,128,1,16,64]{1,0,4,3,2:T(8,128)S(1)} %bitcast.570, f32[8,16,64,128]{3,2,1,0:T(8,128)S(1)} %copy-done.11), kind=kLoop, calls=%fused_computation.41 | loop fusion | flops 4161536 | bytes 12713984 | tf_op jit(solution)/shard_map/transpose(jvp())/reduce_sum | solution.py:176
  130.0 11.5 %fusion.6 = (f32[8,16,128]{2,1,0:T(8,128)}, f32[8,16,128]{2,1,0:T(8,128)}, f32[8,128,128]{2,1,0:T(8,128)}) fusion(f32[8,128,128]{2,1,0:T(8,128)S(1)} %copy-done.43, f32[8,16,128]{2,1,0:T(8,128)S(1)} %bitcast.594, pred[128,128]{1,0:T(8,128)(4,1)S(1)} %copy-done.55, bf16[8,128,16,64]{1,0,3,2:T(8,128)(2,1)S(1)} %bitcast.602, f32[8,16,64,128]{3,0,2,1:T(8,128)S(1)} %bitcast.571), kind=kOutput, calls=%fused_computation.10 | convolution fusion | flops 824016896 | bytes 7553024 | tf_op jit(solution)/shard_map/transpose(jvp(kgrij,kjgrp->kigrp))/dot_general | solution.py:145
  141.5 4.1 %copy.117 = bf16[1024,1024]{1,0:T(8,128)(2,1)} copy(bf16[1024,1024]{0,1:T(8,128)(2,1)} %get-tuple-element.79) | data formatting | bytes 4194304
  145.6 2.5 %copy.115 = bf16[1024,1024]{1,0:T(8,128)(2,1)} copy(bf16[1024,1024]{0,1:T(8,128)(2,1)S(1)} %copy-done.17) | data formatting | bytes 4194304
  148.2 2.3 multiply_reduce_fusion.9
  150.5 2.1 multiply_reduce_fusion.8
  152.6 1.5 multiply_reduce_fusion.7
  154.5 1.7 multiply_reduce_fusion.10
  156.5 4.3 %fusion.71 = f32[8,128,1,128]{1,3,0,2:T(8,128)} fusion(f32[8,128,16,64]{1,0,3,2:T(8,128)S(1)} %copy-done.15, f32[1,1,16,64,128]{4,3,2,1,0:T(8,128)S(1)} %get-tuple-element.84, f32[1,1,16,64,128]{4,3,2,1,0:T(8,128)S(1)} %bitcast.614, f32[1,1,16,64,128]{4,3,2,1,0:T(8,128)S(1)} %bitcast.612, f32[1,1,16,64,128]{4,3,2,1,0:T(8,128)S(1)} %bitcast.610, ...), kind=kOutput, calls=%fused_computation.93 | convolution fusion | flops 811597824 | bytes 8388608 | tf_op jit(solution)/shard_map/transpose(jvp(kjgrp,kjgn->kgrpn))/dot_general | solution.py:126
  160.8 2.3 fusion.21
  163.3 7.5 %bitcast_add_fusion = f32[8,128,1,16,64]{1,4,3,0,2:T(8,128)} fusion(f32[8,16,64,128]{3,2,1,0:T(8,128)S(1)} %get-tuple-element.144, f32[8,128,16]{1,2,0:T(8,128)S(1)} %copy-done.49, f32[8,128,128]{2,1,0:T(8,128)S(1)} %copy-done.44, f32[8,16,128]{2,1,0:T(8,128)S(1)} %bitcast.595, pred[128,128]{1,0:T(8,128)(4,1)S(1)} %copy-done.56, ...), kind=kOutput, calls=%fused_computation.22 | convolution fusion | flops 813694976 | bytes 13254656 | tf_op jit(solution)/shard_map/transpose(jvp(kgrij,kjgrp->kigrp))/dot_general | solution.py:145
  171.6 7.2 %fusion.76 = f32[8,128,1,128]{3,1,0,2:T(8,128)S(1)} fusion(f32[8,1,16,64,128]{4,3,2,1,0:T(8,128)} %copy-done.8, f32[8,128,1,16,64]{1,0,4,3,2:T(8,128)} %bitcast.572, f32[8,128,16]{1,2,0:T(8,128)S(1)} %copy-done.40), kind=kOutput, calls=%fused_computation.94 | convolution fusion | flops 806354944 | bytes 8978432 | tf_op jit(solution)/shard_map/transpose(jvp(kign,kgrpn->kigrp))/dot_general | solution.py:146
  178.8 1.9 fusion.111
  180.8 1.9 collective-permute-start.13
  182.7 1.2 collective-permute-start.12
  183.8 1.5 collective-permute-start.14
  185.7 4.3 %fusion.87 = f32[8,128,1,128]{3,1,0,2:T(8,128)} fusion(f32[8,128,1,128]{3,1,0,2:T(8,128)S(1)} %fusion.92, f32[8,128,1,16,64]{1,0,4,3,2:T(8,128)S(1)} %bitcast.574, f32[8,128,16]{1,2,0:T(8,128)S(1)} %copy-done.38, f32[1,16,64,128]{3,2,1,0:T(8,128)S(1)} %fusion.101), kind=kOutput, calls=%fused_computation.100 | convolution fusion | flops 806486016 | bytes 5832704 | tf_op jit(solution)/shard_map/transpose(jvp(kign,grpn->kigrp))/dot_general | solution.py:175
  190.0 3.1 %collective-permute-done.13 = f32[1,16,64,128]{3,2,1,0:T(8,128)S(1)} collective-permute-done((f32[1,16,64,128]{3,2,1,0:T(8,128)S(1)}, f32[1,16,64,128]{3,2,1,0:T(8,128)S(1)}, u32[]{:S(2)}, u32[]{:S(2)}) %collective-permute-start.13) | collective-permute-done | bytes 524320 | tf_op jit(solution)/shard_map/ppermute | solution.py:40
  193.0 14.4 %collective-permute-done.12 = f32[1,16,64,128]{3,2,1,0:T(8,128)S(1)} collective-permute-done((f32[1,16,64,128]{3,2,1,0:T(8,128)S(1)}, f32[1,16,64,128]{3,2,1,0:T(8,128)S(1)}, u32[]{:S(2)}, u32[]{:S(2)}) %collective-permute-start.12) | collective-permute-done | bytes 524320 | tf_op jit(solution)/shard_map/ppermute | solution.py:40
  207.5 2.2 multiply_reduce_fusion.3
  209.7 1.4 fusion.81
  211.1 1.8 fusion.16
  212.9 1.2 fusion.94
  214.2 3.0 %copy.138 = f32[128,8,8,128]{3,2,1,0:T(8,128)} copy(f32[128,8,8,128]{3,1,2,0:T(8,128)S(1)} %bitcast.584) | data formatting | bytes 8388608
  218.0 1.0 copy.113
  219.7 4.5 %fusion.32 = bf16[8,128,1,16,64]{1,4,3,0,2:T(8,128)(2,1)S(1)} fusion(f32[8,128,1,16,64]{1,4,3,0,2:T(8,128)} %bitcast_add_fusion, f32[8,128,1,16,64]{1,0,2,4,3:T(8,128)} %bitcast.583), kind=kLoop, calls=%fused_computation.51 | loop fusion | flops 2097152 | bytes 10485760 | tf_op jit(solution)/shard_map/convert_element_type | solution.py:257
  224.2 4.2 %copy.128 = bf16[8,128,1,16,64]{4,3,1,0,2:T(8,128)(2,1)} copy(bf16[8,128,1,16,64]{1,4,3,0,2:T(8,128)(2,1)S(1)} %fusion.32) | data formatting | bytes 4194304
  228.4 6.5 %reshape.1403 = bf16[1024,1024]{1,0:T(8,128)(2,1)} reshape(bf16[8,128,1,16,64]{4,3,1,0,2:T(8,128)(2,1)} %copy.128) | data formatting | bytes 4194304
  (273 shorter events, 25.6 us)
Async XLA Ops:
  0.6 26.8 %copy-start = (bf16[1024,1,128]{2,0,1:T(8,128)(2,1)S(1)}, bf16[1024,1,128]{2,0,1:T(8,128)(2,1)}, u32[]{:S(2)}) copy-start(bf16[1024,1,128]{2,0,1:T(8,128)(2,1)} %param.11) | copy-start | bytes 786436
  4.4 20.4 %copy-start.48 = (f32[8,128,16]{1,2,0:T(8,128)}, f32[8,128,16]{1,2,0:T(8,128)S(1)}, u32[]{:S(2)}) copy-start(f32[8,128,16]{1,2,0:T(8,128)S(1)} %get-tuple-element.96) | copy-start | bytes 196612
  4.4 34.5 %copy-start.39 = (f32[8,128,16]{1,2,0:T(8,128)}, f32[8,128,16]{1,2,0:T(8,128)S(1)}, u32[]{:S(2)}) copy-start(f32[8,128,16]{1,2,0:T(8,128)S(1)} %get-tuple-element.95) | copy-start | bytes 196612
  10.3 13.9 %copy-start.33 = (f32[1,16,8,128]{3,2,1,0:T(8,128)}, f32[1,16,8,128]{3,2,1,0:T(8,128)S(1)}, u32[]{:S(2)}) copy-start(f32[1,16,8,128]{3,2,1,0:T(8,128)S(1)} %broadcast_in_dim.280) | copy-start | bytes 196612
  11.4 46.6 %collective-permute-start.1 = (f32[1,16,72,128]{3,2,1,0:T(8,128)}, f32[1,16,72,128]{3,2,1,0:T(8,128)}, u32[]{:S(2)}, u32[]{:S(2)}) collective-permute-start(f32[1,16,72,128]{3,2,1,0:T(8,128)} %get-tuple-element.90), channel_id=1, source_target_pairs={{0,16},{8,24},{16,0},{24,8},{32,48},{40,56},{48,32},{56,40},{64,80... | collective-permute-start | bytes 1769480 | tf_op jit(solution)/shard_map/ppermute | solution.py:40
  15.0 43.0 %collective-permute-start = (f32[1,16,72,128]{3,2,1,0:T(8,128)}, f32[1,16,72,128]{3,2,1,0:T(8,128)}, u32[]{:S(2)}, u32[]{:S(2)}) collective-permute-start(f32[1,16,72,128]{3,2,1,0:T(8,128)} %get-tuple-element.90), channel_id=1, source_target_pairs={{0,8},{8,16},{16,24},{24,0},{32,40},{40,48},{48,56},{56,32},{64,72... | collective-permute-start | bytes 1769480 | tf_op jit(solution)/shard_map/ppermute | solution.py:40
  15.3 42.7 %collective-permute-start.2 = (f32[1,16,72,128]{3,2,1,0:T(8,128)}, f32[1,16,72,128]{3,2,1,0:T(8,128)}, u32[]{:S(2)}, u32[]{:S(2)}) collective-permute-start(f32[1,16,72,128]{3,2,1,0:T(8,128)} %get-tuple-element.90), channel_id=1, source_target_pairs={{0,24},{8,0},{16,8},{24,16},{32,56},{40,32},{48,40},{56,48},{64,88... | collective-permute-start | bytes 1769480 | tf_op jit(solution)/shard_map/ppermute | solution.py:40
  18.9 20.0 %copy-start.54 = (pred[128,128]{1,0:T(8,128)(4,1)}, pred[128,128]{1,0:T(8,128)(4,1)S(1)}, u32[]{:S(2)}) copy-start(pred[128,128]{1,0:T(8,128)(4,1)S(1)} %iota_compare_fusion.6) | copy-start | bytes 49156
  24.8 9.8 %copy-start.58 = (f32[16]{0:T(128)}, f32[16]{0:T(128)S(1)}, u32[]{:S(2)}) copy-start(f32[16]{0:T(128)S(1)} %get-tuple-element.107) | copy-start | bytes 196
  24.8 10.0 %copy-start.69 = (f32[16]{0:T(128)}, f32[16]{0:T(128)S(1)}, u32[]{:S(2)}) copy-start(f32[16]{0:T(128)S(1)} %get-tuple-element.106) | copy-start | bytes 196
  24.8 10.8 %copy-start.64 = (f32[16]{0:T(128)}, f32[16]{0:T(128)S(1)}, u32[]{:S(2)}) copy-start(f32[16]{0:T(128)S(1)} %get-tuple-element.105) | copy-start | bytes 196
  24.8 10.9 %copy-start.66 = (f32[16]{0:T(128)}, f32[16]{0:T(128)S(1)}, u32[]{:S(2)}) copy-start(f32[16]{0:T(128)S(1)} %get-tuple-element.104) | copy-start | bytes 196
  24.8 11.1 %copy-start.67 = (f32[16]{0:T(128)}, f32[16]{0:T(128)S(1)}, u32[]{:S(2)}) copy-start(f32[16]{0:T(128)S(1)} %get-tuple-element.103) | copy-start | bytes 196
  24.8 11.2 %copy-start.68 = (f32[16]{0:T(128)}, f32[16]{0:T(128)S(1)}, u32[]{:S(2)}) copy-start(f32[16]{0:T(128)S(1)} %get-tuple-element.102) | copy-start | bytes 196
  25.5 13.4 %copy-start.30 = (bf16[128,8,8,128]{3,2,1,0:T(8,128)(2,1)}, bf16[128,8,8,128]{3,2,1,0:T(8,128)(2,1)S(1)}, u32[]{:S(2)}) copy-start(bf16[128,8,8,128]{3,2,1,0:T(8,128)(2,1)S(1)} %copy.132) | copy-start | bytes 6291460
  27.7 11.2 %copy-start.42 = (f32[8,128,128]{2,1,0:T(8,128)}, f32[8,128,128]{2,1,0:T(8,128)S(1)}, u32[]{:S(2)}) copy-start(f32[8,128,128]{2,1,0:T(8,128)S(1)} %fusion.171) | copy-start | bytes 1572868
  38.9 8.2 %copy-start.10 = (f32[8,16,64,128]{3,2,1,0:T(8,128)}, f32[8,16,64,128]{3,2,1,0:T(8,128)S(1)}, u32[]{:S(2)}) copy-start(f32[8,16,64,128]{3,2,1,0:T(8,128)S(1)} %fusion.30) | copy-start | bytes 12582916
  48.4 8.3 %copy-start.81 = (pred[4]{0:T(512)(128)(4,1)S(1)}, pred[4]{0:T(512)(128)(4,1)}, u32[]{:S(2)}) copy-start(pred[4]{0:T(512)(128)(4,1)} %get-tuple-element.145) | copy-start | bytes 16
  48.4 9.7 %copy-start.29 = (f32[1,1,16,72,128]{4,3,2,1,0:T(8,128)S(1)}, f32[1,1,16,72,128]{4,3,2,1,0:T(8,128)}, u32[]{:S(2)}) copy-start(f32[1,1,16,72,128]{4,3,2,1,0:T(8,128)} %get-tuple-element.89) | copy-start | bytes 1769476
  59.2 9.9 %copy-start.83 = (pred[4]{0:T(512)(128)(4,1)S(1)}, pred[4]{0:T(512)(128)(4,1)}, u32[]{:S(2)}) copy-start(pred[4]{0:T(512)(128)(4,1)} %copy-done.82) | copy-start | bytes 16
  59.2 9.8 %copy-start.85 = (pred[4]{0:T(512)(128)(4,1)S(1)}, pred[4]{0:T(512)(128)(4,1)}, u32[]{:S(2)}) copy-start(pred[4]{0:T(512)(128)(4,1)} %copy-done.84) | copy-start | bytes 16
  59.2 33.6 %copy-start.79 = (pred[4,4]{1,0:T(4,128)(4,1)S(1)}, pred[4,4]{1,0:T(4,128)(4,1)}, u32[]{:S(2)}) copy-start(pred[4,4]{1,0:T(4,128)(4,1)} %get-tuple-element.135) | copy-start | bytes 52
  59.2 33.6 %copy-start.80 = (pred[4,4]{1,0:T(4,128)(4,1)S(1)}, pred[4,4]{1,0:T(4,128)(4,1)}, u32[]{:S(2)}) copy-start(pred[4,4]{1,0:T(4,128)(4,1)} %get-tuple-element.136) | copy-start | bytes 52
  59.2 33.7 %copy-start.87 = (pred[4]{0:T(512)(128)(4,1)S(1)}, pred[4]{0:T(512)(128)(4,1)}, u32[]{:S(2)}) copy-start(pred[4]{0:T(512)(128)(4,1)} %get-tuple-element.150) | copy-start | bytes 16
  59.2 33.8 %copy-start.34 = (f32[1,16,8,128]{3,2,1,0:T(8,128)S(1)}, f32[1,16,8,128]{3,2,1,0:T(8,128)}, u32[]{:S(2)}) copy-start(f32[1,16,8,128]{3,2,1,0:T(8,128)} %copy-done.33) | copy-start | bytes 196612
  62.4 32.4 %copy-start.28 = (f32[8,128,1,16,64]{1,4,3,0,2:T(8,128)S(1)}, f32[8,128,1,16,64]{1,4,3,0,2:T(8,128)}, u32[]{:S(2)}) copy-start(f32[8,128,1,16,64]{1,4,3,0,2:T(8,128)} %bitcast_add_fusion.1) | copy-start | bytes 12582916
  62.4 32.4 %copy-start.37 = (f32[8,128,16]{1,2,0:T(8,128)S(1)}, f32[8,128,16]{1,2,0:T(8,128)}, u32[]{:S(2)}) copy-start(f32[8,128,16]{1,2,0:T(8,128)} %get-tuple-element.92) | copy-start | bytes 196612
  62.5 15.9 %collective-permute-start.4 = (f32[1,16,72,128]{3,2,1,0:T(8,128)S(1)}, f32[1,16,72,128]{3,2,1,0:T(8,128)S(1)}, u32[]{:S(2)}, u32[]{:S(2)}) collective-permute-start(f32[1,16,72,128]{3,2,1,0:T(8,128)S(1)} %get-tuple-element.88), channel_id=1, source_target_pairs={{0,64},{32,96},{64,0},{96,32},{8,72},{40,104},{72,8},{104,40},{16,... | collective-permute-start | bytes 1769480 | tf_op jit(solution)/shard_map/ppermute | solution.py:40
  66.2 26.4 %collective-permute-start.3 = (f32[1,16,72,128]{3,2,1,0:T(8,128)S(1)}, f32[1,16,72,128]{3,2,1,0:T(8,128)S(1)}, u32[]{:S(2)}, u32[]{:S(2)}) collective-permute-start(f32[1,16,72,128]{3,2,1,0:T(8,128)S(1)} %get-tuple-element.88), channel_id=1, source_target_pairs={{0,32},{32,64},{64,96},{96,0},{8,40},{40,72},{72,104},{104,8},{16,... | collective-permute-start | bytes 1769480 | tf_op jit(solution)/shard_map/ppermute | solution.py:40
  66.9 25.7 %collective-permute-start.5 = (f32[1,16,72,128]{3,2,1,0:T(8,128)S(1)}, f32[1,16,72,128]{3,2,1,0:T(8,128)S(1)}, u32[]{:S(2)}, u32[]{:S(2)}) collective-permute-start(f32[1,16,72,128]{3,2,1,0:T(8,128)S(1)} %get-tuple-element.88), channel_id=1, source_target_pairs={{0,96},{32,0},{64,32},{96,64},{8,104},{40,8},{72,40},{104,72},{16,... | collective-permute-start | bytes 1769480 | tf_op jit(solution)/shard_map/ppermute | solution.py:40
  99.6 12.1 %copy-start.46 = (f32[2,8,8,128]{3,1,2,0:T(8,128)S(1)}, f32[2,8,8,128]{3,1,2,0:T(8,128)}, u32[]{:S(2)}) copy-start(f32[2,8,8,128]{3,1,2,0:T(8,128)} %copy.207) | copy-start | bytes 196612
  102.5 2.5 %collective-permute-start.6 = (f32[2,1024]{1,0:T(2,128)S(1)}, f32[2,1024]{1,0:T(2,128)S(1)}, u32[]{:S(2)}, u32[]{:S(2)}) collective-permute-start(f32[2,1024]{1,0:T(2,128)S(1)} %pad_maximum_fusion.8), channel_id=1, source_target_pairs={{0,1},{1,0},{2,3},{3,2},{4,5},{5,4},{6,7},{7,6},{8,9},{9,8},{10,11... | collective-permute-start | bytes 24584 | tf_op jit(solution)/shard_map/ppermute | solution.py:96
  105.0 2.6 %collective-permute-start.7 = (f32[2,1024]{1,0:T(2,128)S(1)}, f32[2,1024]{1,0:T(2,128)S(1)}, u32[]{:S(2)}, u32[]{:S(2)}) collective-permute-start(f32[2,1024]{1,0:T(2,128)S(1)} %fusion.163), channel_id=1, source_target_pairs={{0,2},{1,3},{2,0},{3,1},{4,6},{5,7},{6,4},{7,5},{8,10},{9,11},{10,... | collective-permute-start | bytes 24584 | tf_op jit(solution)/shard_map/ppermute | solution.py:96
  107.6 4.1 %collective-permute-start.8 = (f32[2,1024]{1,0:T(2,128)S(1)}, f32[2,1024]{1,0:T(2,128)S(1)}, u32[]{:S(2)}, u32[]{:S(2)}) collective-permute-start(f32[2,1024]{1,0:T(2,128)S(1)} %fusion.184), channel_id=1, source_target_pairs={{0,4},{1,5},{2,6},{3,7},{4,0},{5,1},{6,2},{7,3},{8,12},{9,13},{10,... | collective-permute-start | bytes 24584 | tf_op jit(solution)/shard_map/ppermute | solution.py:96
  119.2 59.5 %collective-permute-start.11 = (f32[1,16,64,128]{3,2,1,0:T(8,128)}, f32[1,16,64,128]{3,2,1,0:T(8,128)}, u32[]{:S(2)}, u32[]{:S(2)}) collective-permute-start(f32[1,16,64,128]{3,2,1,0:T(8,128)} %bitcast.154), channel_id=1, source_target_pairs={{0,24},{8,0},{16,8},{24,16},{32,56},{40,32},{48,40},{56,48},{64,88... | collective-permute-start | bytes 1572872 | tf_op jit(solution)/shard_map/ppermute | solution.py:40
  119.3 59.5 %collective-permute-start.10 = (f32[1,16,64,128]{3,2,1,0:T(8,128)}, f32[1,16,64,128]{3,2,1,0:T(8,128)}, u32[]{:S(2)}, u32[]{:S(2)}) collective-permute-start(f32[1,16,64,128]{3,2,1,0:T(8,128)} %bitcast.154), channel_id=1, source_target_pairs={{0,16},{8,24},{16,0},{24,8},{32,48},{40,56},{48,32},{56,40},{64,80... | collective-permute-start | bytes 1572872 | tf_op jit(solution)/shard_map/ppermute | solution.py:40
  120.1 58.6 %collective-permute-start.9 = (f32[1,16,64,128]{3,2,1,0:T(8,128)}, f32[1,16,64,128]{3,2,1,0:T(8,128)}, u32[]{:S(2)}, u32[]{:S(2)}) collective-permute-start(f32[1,16,64,128]{3,2,1,0:T(8,128)} %bitcast.154), channel_id=1, source_target_pairs={{0,8},{8,16},{16,24},{24,0},{32,40},{40,48},{48,56},{56,32},{64,72... | collective-permute-start | bytes 1572872 | tf_op jit(solution)/shard_map/ppermute | solution.py:40
  122.0 8.1 %copy-start.1 = (f32[128,8,8,128]{3,2,1,0:T(8,128)}, f32[128,8,8,128]{3,2,1,0:T(8,128)S(1)}, u32[]{:S(2)}) copy-start(f32[128,8,8,128]{3,2,1,0:T(8,128)S(1)} %copy.135) | copy-start | bytes 12582916
  163.2 7.6 %copy-start.41 = (f32[8,128,16]{1,2,0:T(8,128)S(1)}, f32[8,128,16]{1,2,0:T(8,128)}, u32[]{:S(2)}) copy-start(f32[8,128,16]{1,2,0:T(8,128)} %get-tuple-element.39) | copy-start | bytes 196612
  163.2 7.8 %copy-start.88 = (f32[16]{0:T(128)S(1)}, f32[16]{0:T(128)}, u32[]{:S(2)}) copy-start(f32[16]{0:T(128)} %get-tuple-element.60) | copy-start | bytes 196
  163.2 7.8 %copy-start.89 = (f32[16]{0:T(128)S(1)}, f32[16]{0:T(128)}, u32[]{:S(2)}) copy-start(f32[16]{0:T(128)} %get-tuple-element.62) | copy-start | bytes 196
  163.2 7.8 %copy-start.90 = (f32[16]{0:T(128)S(1)}, f32[16]{0:T(128)}, u32[]{:S(2)}) copy-start(f32[16]{0:T(128)} %get-tuple-element.64) | copy-start | bytes 196
  163.2 8.0 %copy-start.47 = (f32[8,128,16]{1,2,0:T(8,128)S(1)}, f32[8,128,16]{1,2,0:T(8,128)}, u32[]{:S(2)}) copy-start(f32[8,128,16]{1,2,0:T(8,128)} %get-tuple-element.40) | copy-start | bytes 196612
  163.2 8.0 %copy-start.52 = (f32[8,16,128]{2,1,0:T(8,128)S(1)}, f32[8,16,128]{2,1,0:T(8,128)}, u32[]{:S(2)}) copy-start(f32[8,16,128]{2,1,0:T(8,128)} %get-tuple-element.34) | copy-start | bytes 196612
  163.2 8.0 %copy-start.53 = (f32[8,16,128]{2,1,0:T(8,128)S(1)}, f32[8,16,128]{2,1,0:T(8,128)}, u32[]{:S(2)}) copy-start(f32[8,16,128]{2,1,0:T(8,128)} %get-tuple-element.35) | copy-start | bytes 196612
  171.5 7.3 %copy-start.60 = (f32[16]{0:T(128)S(1)}, f32[16]{0:T(128)}, u32[]{:S(2)}) copy-start(f32[16]{0:T(128)} %get-tuple-element.117) | copy-start | bytes 196
  171.5 7.3 %copy-start.61 = (f32[16]{0:T(128)S(1)}, f32[16]{0:T(128)}, u32[]{:S(2)}) copy-start(f32[16]{0:T(128)} %get-tuple-element.118) | copy-start | bytes 196
  171.5 7.3 %copy-start.62 = (f32[16]{0:T(128)S(1)}, f32[16]{0:T(128)}, u32[]{:S(2)}) copy-start(f32[16]{0:T(128)} %get-tuple-element.119) | copy-start | bytes 196
  171.5 7.3 %copy-start.63 = (f32[16]{0:T(128)S(1)}, f32[16]{0:T(128)}, u32[]{:S(2)}) copy-start(f32[16]{0:T(128)} %get-tuple-element.120) | copy-start | bytes 196
  171.5 13.8 %copy-start.32 = (f32[8,128,128]{2,1,0:T(8,128)S(1)}, f32[8,128,128]{2,1,0:T(8,128)}, u32[]{:S(2)}) copy-start(f32[8,128,128]{2,1,0:T(8,128)} %get-tuple-element.36) | copy-start | bytes 1572868
  180.7 26.8 %copy-start.71 = (f32[16]{0:T(128)S(1)}, f32[16]{0:T(128)}, u32[]{:S(2)}) copy-start(f32[16]{0:T(128)} %get-tuple-element.109) | copy-start | bytes 196
  180.7 26.8 %copy-start.72 = (f32[16]{0:T(128)S(1)}, f32[16]{0:T(128)}, u32[]{:S(2)}) copy-start(f32[16]{0:T(128)} %get-tuple-element.110) | copy-start | bytes 196
  180.7 26.7 %copy-start.73 = (f32[16]{0:T(128)S(1)}, f32[16]{0:T(128)}, u32[]{:S(2)}) copy-start(f32[16]{0:T(128)} %get-tuple-element.111) | copy-start | bytes 196
  180.7 26.7 %copy-start.74 = (f32[16]{0:T(128)S(1)}, f32[16]{0:T(128)}, u32[]{:S(2)}) copy-start(f32[16]{0:T(128)} %get-tuple-element.112) | copy-start | bytes 196
  180.7 26.7 %copy-start.75 = (f32[16]{0:T(128)S(1)}, f32[16]{0:T(128)}, u32[]{:S(2)}) copy-start(f32[16]{0:T(128)} %get-tuple-element.113) | copy-start | bytes 196
  180.7 26.7 %copy-start.76 = (f32[16]{0:T(128)S(1)}, f32[16]{0:T(128)}, u32[]{:S(2)}) copy-start(f32[16]{0:T(128)} %get-tuple-element.114) | copy-start | bytes 196
  180.7 26.7 %copy-start.77 = (f32[16]{0:T(128)S(1)}, f32[16]{0:T(128)}, u32[]{:S(2)}) copy-start(f32[16]{0:T(128)} %get-tuple-element.115) | copy-start | bytes 196
  180.8 26.7 %copy-start.78 = (f32[16]{0:T(128)S(1)}, f32[16]{0:T(128)}, u32[]{:S(2)}) copy-start(f32[16]{0:T(128)} %get-tuple-element.116) | copy-start | bytes 196
  180.8 26.7 %copy-start.92 = (f32[16]{0:T(128)S(1)}, f32[16]{0:T(128)}, u32[]{:S(2)}) copy-start(f32[16]{0:T(128)} %exp.181) | copy-start | bytes 196
  180.8 12.3 %collective-permute-start.13 = (f32[1,16,64,128]{3,2,1,0:T(8,128)S(1)}, f32[1,16,64,128]{3,2,1,0:T(8,128)S(1)}, u32[]{:S(2)}, u32[]{:S(2)}) collective-permute-start(f32[1,16,64,128]{3,2,1,0:T(8,128)S(1)} %fusion.111), channel_id=1, source_target_pairs={{0,64},{32,96},{64,0},{96,32},{8,72},{40,104},{72,8},{104,40},{16,... | collective-permute-start | bytes 1572872 | tf_op jit(solution)/shard_map/ppermute | solution.py:40
  182.7 24.8 %collective-permute-start.12 = (f32[1,16,64,128]{3,2,1,0:T(8,128)S(1)}, f32[1,16,64,128]{3,2,1,0:T(8,128)S(1)}, u32[]{:S(2)}, u32[]{:S(2)}) collective-permute-start(f32[1,16,64,128]{3,2,1,0:T(8,128)S(1)} %fusion.111), channel_id=1, source_target_pairs={{0,32},{32,64},{64,96},{96,0},{8,40},{40,72},{72,104},{104,8},{16,... | collective-permute-start | bytes 1572872 | tf_op jit(solution)/shard_map/ppermute | solution.py:40
  183.8 23.6 %collective-permute-start.14 = (f32[1,16,64,128]{3,2,1,0:T(8,128)S(1)}, f32[1,16,64,128]{3,2,1,0:T(8,128)S(1)}, u32[]{:S(2)}, u32[]{:S(2)}) collective-permute-start(f32[1,16,64,128]{3,2,1,0:T(8,128)S(1)} %fusion.111), channel_id=1, source_target_pairs={{0,96},{32,0},{64,32},{96,64},{8,104},{40,8},{72,40},{104,72},{16,... | collective-permute-start | bytes 1572872 | tf_op jit(solution)/shard_map/ppermute | solution.py:40
  185.7 24.1 %copy-start.4 = (f32[1024,1024]{0,1:T(8,128)S(1)}, f32[1024,1024]{0,1:T(8,128)}, u32[]{:S(2)}) copy-start(f32[1024,1024]{0,1:T(8,128)} %get-tuple-element.85) | copy-start | bytes 12582916
  185.7 24.1 %copy-start.36 = (f32[2,8,8,128]{3,1,2,0:T(8,128)S(1)}, f32[2,8,8,128]{3,1,2,0:T(8,128)}, u32[]{:S(2)}) copy-start(f32[2,8,8,128]{3,1,2,0:T(8,128)} %copy-done.35) | copy-start | bytes 196612
  (44 other events, 149.5 us)

commit v2 on v0

--- a/solution.py
+++ b/solution.py
@@ -32,11 +32,16 @@
     return jnp.broadcast_to(log_carry[..., None, None], like.shape[:2] + (8, like.shape[3]))
 
 
-def grouped_gather(value, groups, place):
+def grouped_gather(value, groups, place, keep=None):
     size = len(groups[0])
     parts = [value]
     for shift in range(1, size):
-        pairs = [(g[k], g[(k + shift) % size]) for g in groups for k in range(size)]
+        ks = range(size)
+        if keep == "earlier":
+            ks = [k for k in ks if k + shift < size]
+        elif keep == "later":
+            ks = [k for k in ks if k + shift >= size]
+        pairs = [(g[k], g[(k + shift) % size]) for g in groups for k in ks]
         parts.append(lax.ppermute(value, "seq", pairs))
     sources = (place - jnp.arange(size)) % size
     return jnp.stack(parts), sources
@@ -63,7 +68,9 @@
     row_total = weighted_sum(gap_weights(row_logs, ROW, False, row_ids), row_all)[:, :, :size]
     row_log = jnp.sum(row_logs, axis=0)
     col_all, col_ids = grouped_gather(
-        jnp.concatenate([row_total, tile_logs(row_log, final)], axis=2), col_groups, row
+        jnp.concatenate([row_total, tile_logs(row_log, final)], axis=2),
+        col_groups,
+        row,
     )
     col_logs = jnp.max(col_all[:, :, :, size:], axis=(3, 4))
     before_row = weighted_sum(gap_weights(col_logs, row, False, col_ids), col_all)[:, :, :size]
@@ -80,7 +87,7 @@
     row_all = grouped_gather(leaving, row_groups, col)[0]
     in_row = weighted_sum(gap_weights(row_logs, col, True, row_ids), row_all)
     row_head = weighted_sum(gap_weights(row_logs, -1, True, row_ids), row_all)
-    col_all = grouped_gather(row_head, col_groups, row)[0]
+    col_all = grouped_gather(row_head, col_groups, row, "later")[0]
     after_row = weighted_sum(gap_weights(col_logs, row, True, col_ids), col_all)
     out_of_row = jnp.sum(jnp.where((row_ids > col)[:, None, None], row_logs, 0.0), axis=0)
     return in_row + jnp.exp(out_of_row)[..., None, None] * after_row

time: 240 us -> 242 us (level)
  the two profiles are of different devices: /device:TPU:1 before, /device:TPU:47 now
where the time goes in v2:
time: 242 us; the launch traced here: 238 us
  matrix products  63.9 us (26%)
  local copies, waits for them, and re-layouts  56.3 us (23%)
  other arithmetic  48.6 us (20%)
  waiting for transfers between devices  45.7 us (19%)
  starting transfers between devices  21.4 us (9%)
    unnamed x193, local copies, waits for them, and re-layouts  45.9 us
    ppermute x12, waiting for transfers between devices, grouped_gather(): parts.append(lax.ppermute(value, 'seq', pairs))  42 us
    dot_general x3, matrix products, local_core(): jnp.einsum('kgrij,kjgrp->kigrp', weighted, x_blocks, precision=PRECISION)  27.7 us
    ppermute x12, starting transfers between devices, grouped_gather(): parts.append(lax.ppermute(value, 'seq', pairs))  18.3 us
    dot_general x3, matrix products, block_chain(): jnp.einsum('kjgrp,kjgn->kgrpn', scaled, b_blocks, precision=PRECISION)  9.66 us
    dot_general x3, matrix products, local_core(): jnp.einsum('kign,kgrpn->kigrp', c_blocks, starts, precision=PRECISION)  7.66 us
    dot_general x2, matrix products, add_incoming(): jnp.einsum('kign,grpn->kigrp', c_blocks, incoming, precision=PRECISION)  5.88 us
    reduce_sum x5, other arithmetic, block_chain(): carried = factors[block][..., None, None] * carried + block_states[block]  5.82 us
  transfers between devices with their start and end apart: 15, of which 7 were waited for; matrix products, arithmetic and copies ran while one was open for 43% of the time, Pallas kernels for 0%

profile of v2, /device:TPU:47, one launch (start us, length us, event | category | flops | bytes accessed | tf_op | source)
XLA Modules:
  0.0 238.2 jit_solution(16581984638626454305)
XLA Ops:
  4.6 2.9 %copy.80 = bf16[1024,1024]{0,1:T(8,128)(2,1)S(1)} copy(bf16[1024,1024]{1,0:T(8,128)(2,1)} %param.7) | data formatting | bytes 4194304 | tf_op args[0]
  8.4 1.3 convolution_bitcast_fusion.2
  9.8 1.1 fusion.163
  11.1 2.1 collective-permute-start.1
  15.1 4.3 %fusion.165 = (f32[1024,1024]{0,1:T(8,128)}, f32[128,8,8,128]{3,1,2,0:T(8,128)}) fusion(bf16[1024,1024]{0,1:T(8,128)(2,1)S(1)} %copy.80), kind=kLoop, calls=%fused_computation.310 | loop fusion | flops 1048576 | bytes 10485760 | tf_op jit(solution)/shard_map/convert_element_type | solution.py:195
  20.4 5.2 %copy.137 = f32[128,8,8,128]{3,2,1,0:T(8,128)} copy(f32[128,8,8,128]{3,1,2,0:T(8,128)} %get-tuple-element.85) | data formatting | bytes 8388608
  25.6 1.9 copy.136
  27.6 2.6 %broadcast_multiply_fusion.1 = f32[8,128,16,64]{1,0,3,2:T(8,128)S(1)} fusion(f32[8,128,16,64]{1,0,3,2:T(8,128)} %bitcast.583, f32[8,128,16]{1,0,2:T(8,128)S(1)} %copy.83), kind=kLoop, calls=%fused_computation.91 | loop fusion | flops 1048576 | bytes 8454144 | tf_op jit(solution)/shard_map/jvp()/mul | solution.py:132
  30.2 1.6 fusion.53
  32.3 3.1 %copy-done.6 = f32[8,1,16,64,128]{4,3,2,1,0:T(8,128)S(1)} copy-done((f32[8,1,16,64,128]{4,3,2,1,0:T(8,128)S(1)}, f32[8,1,16,64,128]{4,3,2,1,0:T(8,128)}, u32[]{:S(2)}) %copy-start.6) | copy-done | bytes 4194328
  37.7 1.4 fusion.30
  40.8 7.8 %bitcast_add_fusion.1 = f32[8,128,1,16,64]{1,4,3,0,2:T(8,128)} fusion(f32[8,16,64,128]{3,2,1,0:T(8,128)S(1)} %fusion.30, f32[8,128,16]{1,2,0:T(8,128)S(1)} %get-tuple-element.93, f32[8,128,128]{2,1,0:T(8,128)S(1)} %fusion.168, f32[8,16,128]{2,1,0:T(8,128)S(1)} %bitcast.593, pred[128,128]{1,0:T(8,128)(4,1)S(1)} %iota_compare_fusion.6, ...), kind=kOutput, calls=%fused_computation.23 | convolution fusion | flops 813694976 | bytes 11157504 | tf_op jit(solution)/shard_map/jvp(kgrij,kjgrp->kigrp)/dot_general | solution.py:152
  49.2 2.9 %copy.88 = bf16[1024,1024]{0,1:T(8,128)(2,1)S(1)} copy(bf16[1024,1024]{1,0:T(8,128)(2,1)} %param.8) | data formatting | bytes 4194304 | tf_op args[1]
  52.1 3.9 %copy.89 = bf16[1024,1024]{0,1:T(8,128)(2,1)} copy(bf16[1024,1024]{1,0:T(8,128)(2,1)} %param.13) | data formatting | bytes 4194304 | tf_op args[6]
  56.1 1.5 copy.106
  57.6 1.3 compare_and_fusion.5
  58.8 1.3 compare_and_fusion.3
  60.2 1.1 fusion.120
  62.8 1.6 multiply_add_fusion
  64.5 1.7 collective-permute-start.3
  66.3 1.1 collective-permute-start.4
  67.4 2.2 collective-permute-start.5
  71.7 6.6 %collective-permute-done.3 = f32[1,16,72,128]{3,2,1,0:T(8,128)S(1)} collective-permute-done((f32[1,16,72,128]{3,2,1,0:T(8,128)S(1)}, f32[1,16,72,128]{3,2,1,0:T(8,128)S(1)}, u32[]{:S(2)}, u32[]{:S(2)}) %collective-permute-start.3) | collective-permute-done | bytes 589856 | tf_op jit(solution)/shard_map/ppermute | solution.py:45
  78.3 3.0 %collective-permute-done.4 = f32[1,16,72,128]{3,2,1,0:T(8,128)S(1)} collective-permute-done((f32[1,16,72,128]{3,2,1,0:T(8,128)S(1)}, f32[1,16,72,128]{3,2,1,0:T(8,128)S(1)}, u32[]{:S(2)}, u32[]{:S(2)}) %collective-permute-start.4) | collective-permute-done | bytes 589856 | tf_op jit(solution)/shard_map/ppermute | solution.py:45
  81.2 14.1 %collective-permute-done.5 = f32[1,16,72,128]{3,2,1,0:T(8,128)S(1)} collective-permute-done((f32[1,16,72,128]{3,2,1,0:T(8,128)S(1)}, f32[1,16,72,128]{3,2,1,0:T(8,128)S(1)}, u32[]{:S(2)}, u32[]{:S(2)}) %collective-permute-start.5) | collective-permute-done | bytes 589856 | tf_op jit(solution)/shard_map/ppermute | solution.py:45
  95.7 1.7 fusion.102
  97.5 1.6 fusion.23
  99.1 3.3 %copy.87 = f32[8,128,1,16,64]{1,0,4,3,2:T(8,128)S(1)} copy(f32[8,128,1,16,64]{1,4,3,0,2:T(8,128)S(1)} %get-tuple-element.139) | data formatting | bytes 8388608 | tf_op jit(solution)/shard_map/jvp()/add | solution.py:183
  102.5 2.8 %multiply_reduce_fusion.2 = (f32[1024]{0:T(1024)S(1)}, f32[1024]{0:T(1024)S(1)}) fusion(bf16[1024,1024]{0,1:T(8,128)(2,1)S(1)} %copy.88, f32[128,8,8,128]{3,2,1,0:T(8,128)S(1)} %bitcast.579, bf16[1024,1024]{0,1:T(8,128)(2,1)S(1)} %copy-done.9, f32[1024]{0:T(1024)S(1)} %copy-done.52), kind=kLoop, calls=%fused_computation.63 | loop fusion | flops 12580864 | bytes 8400896 | tf_op jit(solution)/shard_map/reduce_sum | solution.py:233
  107.5 2.3 collective-permute-done.7
  109.8 2.1 collective-permute-start.8
  112.5 1.4 collective-permute-done.8
  113.9 5.0 %fusion.12 = (bf16[1024,1024]{0,1:T(8,128)(2,1)}, f32[128,8,8,128]{3,1,2,0:T(8,128)S(1)}, bf16[1024,1024]{0,1:T(8,128)(2,1)}) fusion(bf16[1024,1024]{0,1:T(8,128)(2,1)S(1)} %copy.88, f32[128,8,8,128]{3,2,1,0:T(8,128)S(1)} %bitcast.580, bf16[1024,1024]{0,1:T(8,128)(2,1)S(1)} %copy-done.9, f32[1024]{0:T(1024)S(1)} %fusion.148, f32[1024]{0:T(1024)S(1)} %bitcast.635, ...), kind=kLoop, calls=%fused_computation.16 | loop fusion | flops 23068672 | bytes 16789504 | tf_op jit(solution)/shard_map/convert_element_type | solution.py:243
  119.0 1.0 copy.139
  120.4 2.1 fusion.33
  122.5 2.7 %collective-permute-start.10 = (f32[1,16,64,128]{3,2,1,0:T(8,128)}, f32[1,16,64,128]{3,2,1,0:T(8,128)}, u32[]{:S(2)}, u32[]{:S(2)}) collective-permute-start(f32[1,16,64,128]{3,2,1,0:T(8,128)} %bitcast.153), channel_id=1, source_target_pairs={{0,16},{8,24},{16,0},{24,8},{32,48},{40,56},{48,32},{56,40},{64,80... | collective-permute-start | bytes 1572872 | tf_op jit(solution)/shard_map/ppermute | solution.py:45
  125.7 2.5 %collective-permute-start.9 = (f32[1,16,64,128]{3,2,1,0:T(8,128)}, f32[1,16,64,128]{3,2,1,0:T(8,128)}, u32[]{:S(2)}, u32[]{:S(2)}) collective-permute-start(f32[1,16,64,128]{3,2,1,0:T(8,128)} %bitcast.153), channel_id=1, source_target_pairs={{0,8},{8,16},{16,24},{24,0},{32,40},{40,48},{48,56},{56,32},{64,72... | collective-permute-start | bytes 1572872 | tf_op jit(solution)/shard_map/ppermute | solution.py:45
  128.2 1.6 fusion.19
  133.5 2.4 multiply_reduce_fusion.10
  136.0 2.3 fusion.24
  138.3 4.3 %fusion.72 = f32[8,128,1,128]{1,3,0,2:T(8,128)} fusion(f32[8,128,16,64]{1,0,3,2:T(8,128)S(1)} %copy-done.14, f32[1,1,16,64,128]{4,3,2,1,0:T(8,128)S(1)} %get-tuple-element.83, f32[1,1,16,64,128]{4,3,2,1,0:T(8,128)S(1)} %bitcast.614, f32[1,1,16,64,128]{4,3,2,1,0:T(8,128)S(1)} %bitcast.612, f32[1,1,16,64,128]{4,3,2,1,0:T(8,128)S(1)} %bitcast.610, ...), kind=kOutput, calls=%fused_computation.95 | convolution fusion | flops 811597824 | bytes 8388608 | tf_op jit(solution)/shard_map/transpose(jvp(kjgrp,kjgn->kgrpn))/dot_general | solution.py:133
  142.6 3.8 %fusion.21 = (f32[8,128,16]{1,2,0:T(8,128)S(1)}, f32[8,16,64,128]{3,2,1,0:T(8,128)}) fusion(f32[8,128,1,16,64]{1,0,4,3,2:T(8,128)S(1)} %bitcast.584, bf16[8,128,128,1]{2,1,3,0:T(8,128)(2,1)S(1)} %bitcast.589, f32[1,1,16,64,128]{4,3,2,1,0:T(8,128)S(1)} %get-tuple-element.83, f32[1,1,16,64,128]{4,3,2,1,0:T(8,128)S(1)} %bitcast.615, ...), kind=kOutput, calls=%fused_computation.33 | convolution fusion | flops 813678592 | bytes 12386304 | tf_op jit(solution)/shard_map/transpose(jvp(kjgrp,kjgn->kgrpn))/dot_general | solution.py:133
  149.3 12.5 %fusion.6 = (f32[8,16,128]{2,1,0:T(8,128)S(1)}, f32[8,16,128]{2,1,0:T(8,128)S(1)}, f32[8,128,128]{2,1,0:T(8,128)}) fusion(f32[8,128,128]{2,1,0:T(8,128)} %copy-done.40, f32[8,16,128]{2,1,0:T(8,128)S(1)} %bitcast.595, pred[128,128]{1,0:T(8,128)(4,1)} %copy-done.53, bf16[8,128,16,64]{1,0,3,2:T(8,128)(2,1)S(1)} %bitcast.602, f32[8,16,64,128]{3,0,2,1:T(8,128)} %bitcast.573), kind=kOutput, calls=%fused_computation.10 | convolution fusion | flops 824016896 | bytes 7553024 | tf_op jit(solution)/shard_map/transpose(jvp(kgrij,kjgrp->kigrp))/dot_general | solution.py:152
  161.9 7.4 %bitcast_add_fusion = f32[8,128,1,16,64]{1,4,3,0,2:T(8,128)} fusion(f32[8,16,64,128]{3,2,1,0:T(8,128)S(1)} %copy-done.88, f32[8,128,16]{1,2,0:T(8,128)S(1)} %copy-done.47, f32[8,128,128]{2,1,0:T(8,128)S(1)} %copy-done.41, f32[8,16,128]{2,1,0:T(8,128)S(1)} %bitcast.596, pred[128,128]{1,0:T(8,128)(4,1)S(1)} %copy-done.54, f32[8,16,64,128]{3,0,2,1:T(8,128)S(1)} %bitcast.574), kind=kOutput, calls=%fused_computation.22 | convolution fusion | flops 813694976 | bytes 13254656 | tf_op jit(solution)/shard_map/transpose(jvp(kgrij,kjgrp->kigrp))/dot_general | solution.py:152
  170.2 4.7 %fusion.77 = f32[8,128,1,128]{3,1,0,2:T(8,128)} fusion(f32[8,1,16,64,128]{4,3,2,1,0:T(8,128)S(1)} %copy-done.8, f32[8,128,1,16,64]{1,0,4,3,2:T(8,128)S(1)} %bitcast.575, f32[8,128,16]{1,2,0:T(8,128)S(1)} %copy-done.39), kind=kOutput, calls=%fused_computation.96 | convolution fusion | flops 806354944 | bytes 8978432 | tf_op jit(solution)/shard_map/transpose(jvp(kign,kgrpn->kigrp))/dot_general | solution.py:153
  174.9 4.1 %copy.118 = bf16[1024,1024]{1,0:T(8,128)(2,1)} copy(bf16[1024,1024]{0,1:T(8,128)(2,1)} %get-tuple-element.79) | data formatting | bytes 4194304
  179.0 2.5 %copy.120 = bf16[1024,1024]{1,0:T(8,128)(2,1)} copy(bf16[1024,1024]{0,1:T(8,128)(2,1)S(1)} %copy-done.15) | data formatting | bytes 4194304
  181.6 1.9 fusion.112
  184.2 1.3 collective-permute-start.13
  185.5 3.0 %collective-permute-start.14 = (f32[1,16,64,128]{3,2,1,0:T(8,128)S(1)}, f32[1,16,64,128]{3,2,1,0:T(8,128)S(1)}, u32[]{:S(2)}, u32[]{:S(2)}) collective-permute-start(f32[1,16,64,128]{3,2,1,0:T(8,128)S(1)} %fusion.112), channel_id=1, source_target_pairs={{32,0},{64,32},{96,64},{40,8},{72,40},{104,72},{48,16},{80,48},{11... | collective-permute-start | bytes 1572872 | tf_op jit(solution)/shard_map/ppermute | solution.py:45
  188.6 1.5 fusion.93
  190.1 4.3 %fusion.88 = f32[8,128,1,128]{3,1,0,2:T(8,128)} fusion(f32[8,128,1,128]{3,1,0,2:T(8,128)S(1)} %fusion.93, f32[8,128,1,16,64]{1,0,4,3,2:T(8,128)S(1)} %bitcast.576, f32[8,128,16]{1,2,0:T(8,128)S(1)} %copy-done.34, f32[1,16,64,128]{3,2,1,0:T(8,128)S(1)} %fusion.102), kind=kOutput, calls=%fused_computation.102 | convolution fusion | flops 806486016 | bytes 5832704 | tf_op jit(solution)/shard_map/transpose(jvp(kign,grpn->kigrp))/dot_general | solution.py:182
  194.4 3.6 %collective-permute-done.13 = f32[1,16,64,128]{3,2,1,0:T(8,128)S(1)} collective-permute-done((f32[1,16,64,128]{3,2,1,0:T(8,128)S(1)}, f32[1,16,64,128]{3,2,1,0:T(8,128)S(1)}, u32[]{:S(2)}, u32[]{:S(2)}) %collective-permute-start.13) | collective-permute-done | bytes 524320 | tf_op jit(solution)/shard_map/ppermute | solution.py:45
  198.0 14.7 %collective-permute-done.14 = f32[1,16,64,128]{3,2,1,0:T(8,128)S(1)} collective-permute-done((f32[1,16,64,128]{3,2,1,0:T(8,128)S(1)}, f32[1,16,64,128]{3,2,1,0:T(8,128)S(1)}, u32[]{:S(2)}, u32[]{:S(2)}) %collective-permute-start.14) | collective-permute-done | bytes 524320 | tf_op jit(solution)/shard_map/ppermute | solution.py:45
  212.8 2.2 multiply_reduce_fusion.3
  215.0 1.4 fusion.82
  217.2 1.0 copy.116
  218.2 3.8 %fusion.16 = (f32[1024,16]{0,1:T(8,128)S(1)}, f32[1024,1,16,64]{0,3,2,1:T(8,128)S(1)}) fusion(f32[1024,1,16,64]{0,3,2,1:T(8,128)} %bitcast.577, f32[1024,16]{0,1:T(8,128)S(1)} %bitcast.618, bf16[1024,1,128]{2,0,1:T(8,128)(2,1)S(1)} %copy-done.17, f32[1,16,64,128]{3,2,1,0:T(8,128)S(1)} %get-tuple-element.57), kind=kOutput, calls=%fused_computation.26 | convolution fusion | flops 808435712 | bytes 9306112 | tf_op jit(solution)/shard_map/tgn,grpn->tgrp/dot_general | solution.py:166
  222.0 1.2 fusion.95
  224.0 1.0 copy.142
  225.0 1.2 copy-done.29
  226.2 1.1 fusion.32
  227.3 4.2 %copy.132 = bf16[8,128,1,16,64]{4,3,1,0,2:T(8,128)(2,1)} copy(bf16[8,128,1,16,64]{1,4,3,0,2:T(8,128)(2,1)S(1)} %fusion.32) | data formatting | bytes 4194304
  231.5 6.5 %reshape.1395 = bf16[1024,1024]{1,0:T(8,128)(2,1)} reshape(bf16[8,128,1,16,64]{4,3,1,0,2:T(8,128)(2,1)} %copy.132) | data formatting | bytes 4194304
  (265 shorter events, 30.4 us)
Async XLA Ops:
  0.6 37.1 %copy-start = (bf16[1024,1,128]{2,0,1:T(8,128)(2,1)S(1)}, bf16[1024,1,128]{2,0,1:T(8,128)(2,1)}, u32[]{:S(2)}) copy-start(bf16[1024,1,128]{2,0,1:T(8,128)(2,1)} %param.11) | copy-start | bytes 786436
  4.5 15.8 %copy-start.46 = (f32[8,128,16]{1,2,0:T(8,128)}, f32[8,128,16]{1,2,0:T(8,128)S(1)}, u32[]{:S(2)}) copy-start(f32[8,128,16]{1,2,0:T(8,128)S(1)} %get-tuple-element.94) | copy-start | bytes 196612
  4.5 35.7 %copy-start.38 = (f32[8,128,16]{1,2,0:T(8,128)}, f32[8,128,16]{1,2,0:T(8,128)S(1)}, u32[]{:S(2)}) copy-start(f32[8,128,16]{1,2,0:T(8,128)S(1)} %get-tuple-element.93) | copy-start | bytes 196612
  9.8 9.6 %copy-start.35 = (f32[1,16,8,128]{3,2,1,0:T(8,128)}, f32[1,16,8,128]{3,2,1,0:T(8,128)S(1)}, u32[]{:S(2)}) copy-start(f32[1,16,8,128]{3,2,1,0:T(8,128)S(1)} %broadcast_in_dim.281) | copy-start | bytes 196612
  10.9 49.3 %collective-permute-start = (f32[1,16,72,128]{3,2,1,0:T(8,128)}, f32[1,16,72,128]{3,2,1,0:T(8,128)}, u32[]{:S(2)}, u32[]{:S(2)}) collective-permute-start(f32[1,16,72,128]{3,2,1,0:T(8,128)} %get-tuple-element.89), channel_id=1, source_target_pairs={{0,8},{8,16},{16,24},{24,0},{32,40},{40,48},{48,56},{56,32},{64,72... | collective-permute-start | bytes 1769480 | tf_op jit(solution)/shard_map/ppermute | solution.py:45
  11.1 49.1 %collective-permute-start.1 = (f32[1,16,72,128]{3,2,1,0:T(8,128)}, f32[1,16,72,128]{3,2,1,0:T(8,128)}, u32[]{:S(2)}, u32[]{:S(2)}) collective-permute-start(f32[1,16,72,128]{3,2,1,0:T(8,128)} %get-tuple-element.89), channel_id=1, source_target_pairs={{0,16},{8,24},{16,0},{24,8},{32,48},{40,56},{48,32},{56,40},{64,80... | collective-permute-start | bytes 1769480 | tf_op jit(solution)/shard_map/ppermute | solution.py:45
  13.2 47.0 %collective-permute-start.2 = (f32[1,16,72,128]{3,2,1,0:T(8,128)}, f32[1,16,72,128]{3,2,1,0:T(8,128)}, u32[]{:S(2)}, u32[]{:S(2)}) collective-permute-start(f32[1,16,72,128]{3,2,1,0:T(8,128)} %get-tuple-element.89), channel_id=1, source_target_pairs={{0,24},{8,0},{16,8},{24,16},{32,56},{40,32},{48,40},{56,48},{64,88... | collective-permute-start | bytes 1769480 | tf_op jit(solution)/shard_map/ppermute | solution.py:45
  20.3 19.9 %copy-start.53 = (pred[128,128]{1,0:T(8,128)(4,1)}, pred[128,128]{1,0:T(8,128)(4,1)S(1)}, u32[]{:S(2)}) copy-start(pred[128,128]{1,0:T(8,128)(4,1)S(1)} %iota_compare_fusion.6) | copy-start | bytes 49156
  25.6 9.9 %copy-start.55 = (f32[16]{0:T(128)}, f32[16]{0:T(128)S(1)}, u32[]{:S(2)}) copy-start(f32[16]{0:T(128)S(1)} %get-tuple-element.105) | copy-start | bytes 196
  25.6 10.1 %copy-start.69 = (f32[16]{0:T(128)}, f32[16]{0:T(128)S(1)}, u32[]{:S(2)}) copy-start(f32[16]{0:T(128)S(1)} %get-tuple-element.104) | copy-start | bytes 196
  25.6 10.9 %copy-start.61 = (f32[16]{0:T(128)}, f32[16]{0:T(128)S(1)}, u32[]{:S(2)}) copy-start(f32[16]{0:T(128)S(1)} %get-tuple-element.103) | copy-start | bytes 196
  25.6 11.0 %copy-start.63 = (f32[16]{0:T(128)}, f32[16]{0:T(128)S(1)}, u32[]{:S(2)}) copy-start(f32[16]{0:T(128)S(1)} %get-tuple-element.102) | copy-start | bytes 196
  25.6 11.2 %copy-start.65 = (f32[16]{0:T(128)}, f32[16]{0:T(128)S(1)}, u32[]{:S(2)}) copy-start(f32[16]{0:T(128)S(1)} %get-tuple-element.101) | copy-start | bytes 196
  25.6 11.3 %copy-start.67 = (f32[16]{0:T(128)}, f32[16]{0:T(128)S(1)}, u32[]{:S(2)}) copy-start(f32[16]{0:T(128)S(1)} %get-tuple-element.100) | copy-start | bytes 196
  30.1 5.2 %copy-start.6 = (f32[8,1,16,64,128]{4,3,2,1,0:T(8,128)S(1)}, f32[8,1,16,64,128]{4,3,2,1,0:T(8,128)}, u32[]{:S(2)}) copy-start(f32[8,1,16,64,128]{4,3,2,1,0:T(8,128)} %broadcast_dynamic-update-slice_fusion) | copy-start | bytes 12582916
  39.9 8.8 %copy-start.10 = (f32[8,16,64,128]{3,2,1,0:T(8,128)}, f32[8,16,64,128]{3,2,1,0:T(8,128)S(1)}, u32[]{:S(2)}) copy-start(f32[8,16,64,128]{3,2,1,0:T(8,128)S(1)} %fusion.30) | copy-start | bytes 12582916
  40.2 8.5 %copy-start.40 = (f32[8,128,128]{2,1,0:T(8,128)}, f32[8,128,128]{2,1,0:T(8,128)S(1)}, u32[]{:S(2)}) copy-start(f32[8,128,128]{2,1,0:T(8,128)S(1)} %fusion.168) | copy-start | bytes 1572868
  49.2 9.7 %copy-start.81 = (pred[4]{0:T(512)(128)(4,1)S(1)}, pred[4]{0:T(512)(128)(4,1)}, u32[]{:S(2)}) copy-start(pred[4]{0:T(512)(128)(4,1)} %get-tuple-element.143) | copy-start | bytes 16
  49.2 11.0 %copy-start.30 = (f32[1,1,16,72,128]{4,3,2,1,0:T(8,128)S(1)}, f32[1,1,16,72,128]{4,3,2,1,0:T(8,128)}, u32[]{:S(2)}) copy-start(f32[1,1,16,72,128]{4,3,2,1,0:T(8,128)} %get-tuple-element.88) | copy-start | bytes 1769476
  61.3 34.2 %copy-start.79 = (pred[4,4]{1,0:T(4,128)(4,1)S(1)}, pred[4,4]{1,0:T(4,128)(4,1)}, u32[]{:S(2)}) copy-start(pred[4,4]{1,0:T(4,128)(4,1)} %get-tuple-element.133) | copy-start | bytes 52
  61.3 34.2 %copy-start.80 = (pred[4,4]{1,0:T(4,128)(4,1)S(1)}, pred[4,4]{1,0:T(4,128)(4,1)}, u32[]{:S(2)}) copy-start(pred[4,4]{1,0:T(4,128)(4,1)} %get-tuple-element.134) | copy-start | bytes 52
  61.3 34.3 %copy-start.85 = (pred[4]{0:T(512)(128)(4,1)S(1)}, pred[4]{0:T(512)(128)(4,1)}, u32[]{:S(2)}) copy-start(pred[4]{0:T(512)(128)(4,1)} %copy-done.84) | copy-start | bytes 16
  64.4 33.0 %copy-start.28 = (f32[8,128,1,16,64]{1,4,3,0,2:T(8,128)S(1)}, f32[8,128,1,16,64]{1,4,3,0,2:T(8,128)}, u32[]{:S(2)}) copy-start(f32[8,128,1,16,64]{1,4,3,0,2:T(8,128)} %bitcast_add_fusion.1) | copy-start | bytes 12582916
  64.4 33.0 %copy-start.34 = (f32[8,128,16]{1,2,0:T(8,128)S(1)}, f32[8,128,16]{1,2,0:T(8,128)}, u32[]{:S(2)}) copy-start(f32[8,128,16]{1,2,0:T(8,128)} %get-tuple-element.92) | copy-start | bytes 196612
  64.5 13.7 %collective-permute-start.3 = (f32[1,16,72,128]{3,2,1,0:T(8,128)S(1)}, f32[1,16,72,128]{3,2,1,0:T(8,128)S(1)}, u32[]{:S(2)}, u32[]{:S(2)}) collective-permute-start(f32[1,16,72,128]{3,2,1,0:T(8,128)S(1)} %get-tuple-element.87), channel_id=1, source_target_pairs={{0,32},{32,64},{64,96},{96,0},{8,40},{40,72},{72,104},{104,8},{16,... | collective-permute-start | bytes 1769480 | tf_op jit(solution)/shard_map/ppermute | solution.py:45
  66.3 15.0 %collective-permute-start.4 = (f32[1,16,72,128]{3,2,1,0:T(8,128)S(1)}, f32[1,16,72,128]{3,2,1,0:T(8,128)S(1)}, u32[]{:S(2)}, u32[]{:S(2)}) collective-permute-start(f32[1,16,72,128]{3,2,1,0:T(8,128)S(1)} %get-tuple-element.87), channel_id=1, source_target_pairs={{0,64},{32,96},{64,0},{96,32},{8,72},{40,104},{72,8},{104,40},{16,... | collective-permute-start | bytes 1769480 | tf_op jit(solution)/shard_map/ppermute | solution.py:45
  67.4 27.9 %collective-permute-start.5 = (f32[1,16,72,128]{3,2,1,0:T(8,128)S(1)}, f32[1,16,72,128]{3,2,1,0:T(8,128)S(1)}, u32[]{:S(2)}, u32[]{:S(2)}) collective-permute-start(f32[1,16,72,128]{3,2,1,0:T(8,128)S(1)} %get-tuple-element.87), channel_id=1, source_target_pairs={{0,96},{32,0},{64,32},{96,64},{8,104},{40,8},{72,40},{104,72},{16,... | collective-permute-start | bytes 1769480 | tf_op jit(solution)/shard_map/ppermute | solution.py:45
  105.3 1.9 collective-permute-start.6
  107.2 2.6 %collective-permute-start.7 = (f32[2,1024]{1,0:T(2,128)S(1)}, f32[2,1024]{1,0:T(2,128)S(1)}, u32[]{:S(2)}, u32[]{:S(2)}) collective-permute-start(f32[2,1024]{1,0:T(2,128)S(1)} %fusion.161), channel_id=1, source_target_pairs={{0,2},{1,3},{2,0},{3,1},{4,6},{5,7},{6,4},{7,5},{8,10},{9,11},{10,... | collective-permute-start | bytes 24584 | tf_op jit(solution)/shard_map/ppermute | solution.py:103
  109.8 4.1 %collective-permute-start.8 = (f32[2,1024]{1,0:T(2,128)S(1)}, f32[2,1024]{1,0:T(2,128)S(1)}, u32[]{:S(2)}, u32[]{:S(2)}) collective-permute-start(f32[2,1024]{1,0:T(2,128)S(1)} %fusion.181), channel_id=1, source_target_pairs={{0,4},{1,5},{2,6},{3,7},{4,0},{5,1},{6,2},{7,3},{8,12},{9,13},{10,... | collective-permute-start | bytes 24584 | tf_op jit(solution)/shard_map/ppermute | solution.py:103
  120.0 16.0 %copy-start.1 = (f32[128,8,8,128]{3,2,1,0:T(8,128)}, f32[128,8,8,128]{3,2,1,0:T(8,128)S(1)}, u32[]{:S(2)}) copy-start(f32[128,8,8,128]{3,2,1,0:T(8,128)S(1)} %copy.139) | copy-start | bytes 12582916
  120.4 7.8 %copy-start.39 = (f32[8,128,16]{1,2,0:T(8,128)S(1)}, f32[8,128,16]{1,2,0:T(8,128)}, u32[]{:S(2)}) copy-start(f32[8,128,16]{1,2,0:T(8,128)} %copy-done.38) | copy-start | bytes 196612
  122.5 59.0 %collective-permute-start.10 = (f32[1,16,64,128]{3,2,1,0:T(8,128)}, f32[1,16,64,128]{3,2,1,0:T(8,128)}, u32[]{:S(2)}, u32[]{:S(2)}) collective-permute-start(f32[1,16,64,128]{3,2,1,0:T(8,128)} %bitcast.153), channel_id=1, source_target_pairs={{0,16},{8,24},{16,0},{24,8},{32,48},{40,56},{48,32},{56,40},{64,80... | collective-permute-start | bytes 1572872 | tf_op jit(solution)/shard_map/ppermute | solution.py:45
  125.2 56.3 %collective-permute-start.11 = (f32[1,16,64,128]{3,2,1,0:T(8,128)}, f32[1,16,64,128]{3,2,1,0:T(8,128)}, u32[]{:S(2)}, u32[]{:S(2)}) collective-permute-start(f32[1,16,64,128]{3,2,1,0:T(8,128)} %bitcast.153), channel_id=1, source_target_pairs={{0,24},{8,0},{16,8},{24,16},{32,56},{40,32},{48,40},{56,48},{64,88... | collective-permute-start | bytes 1572872 | tf_op jit(solution)/shard_map/ppermute | solution.py:45
  125.7 55.8 %collective-permute-start.9 = (f32[1,16,64,128]{3,2,1,0:T(8,128)}, f32[1,16,64,128]{3,2,1,0:T(8,128)}, u32[]{:S(2)}, u32[]{:S(2)}) collective-permute-start(f32[1,16,64,128]{3,2,1,0:T(8,128)} %bitcast.153), channel_id=1, source_target_pairs={{0,8},{8,16},{16,24},{24,0},{32,40},{40,48},{48,56},{56,32},{64,72... | collective-permute-start | bytes 1572872 | tf_op jit(solution)/shard_map/ppermute | solution.py:45
  142.6 6.7 %copy-start.32 = (bf16[128,8,8,128]{3,2,1,0:T(8,128)(2,1)S(1)}, bf16[128,8,8,128]{3,2,1,0:T(8,128)(2,1)}, u32[]{:S(2)}) copy-start(bf16[128,8,8,128]{3,2,1,0:T(8,128)(2,1)} %copy.136) | copy-start | bytes 6291460
  149.3 12.6 %copy-start.2 = (f32[128,8,8,128]{3,2,1,0:T(8,128)S(1)}, f32[128,8,8,128]{3,2,1,0:T(8,128)}, u32[]{:S(2)}) copy-start(f32[128,8,8,128]{3,2,1,0:T(8,128)} %copy-done.1) | copy-start | bytes 12582916
  149.3 12.6 %copy-start.41 = (f32[8,128,128]{2,1,0:T(8,128)S(1)}, f32[8,128,128]{2,1,0:T(8,128)}, u32[]{:S(2)}) copy-start(f32[8,128,128]{2,1,0:T(8,128)} %copy-done.40) | copy-start | bytes 1572868
  149.3 12.6 %copy-start.47 = (f32[8,128,16]{1,2,0:T(8,128)S(1)}, f32[8,128,16]{1,2,0:T(8,128)}, u32[]{:S(2)}) copy-start(f32[8,128,16]{1,2,0:T(8,128)} %copy-done.46) | copy-start | bytes 196612
  149.3 12.5 %copy-start.54 = (pred[128,128]{1,0:T(8,128)(4,1)S(1)}, pred[128,128]{1,0:T(8,128)(4,1)}, u32[]{:S(2)}) copy-start(pred[128,128]{1,0:T(8,128)(4,1)} %copy-done.53) | copy-start | bytes 49156
  149.3 12.5 %copy-start.88 = (f32[8,16,64,128]{3,2,1,0:T(8,128)S(1)}, f32[8,16,64,128]{3,2,1,0:T(8,128)}, u32[]{:S(2)}) copy-start(f32[8,16,64,128]{3,2,1,0:T(8,128)} %get-tuple-element.142) | copy-start | bytes 12582916
  161.9 7.4 %copy-start.50 = (f32[8,128,16]{1,2,0:T(8,128)S(1)}, f32[8,128,16]{1,2,0:T(8,128)}, u32[]{:S(2)}) copy-start(f32[8,128,16]{1,2,0:T(8,128)} %copy-done.49) | copy-start | bytes 196612
  161.9 7.4 %copy-start.51 = (f32[8,1,16,1]{3,2,0,1:T(8,128)S(1)}, f32[8,1,16,1]{3,2,0,1:T(8,128)}, u32[]{:S(2)}) copy-start(f32[8,1,16,1]{3,2,0,1:T(8,128)} %copy.104) | copy-start | bytes 1540
  161.9 8.3 %copy-start.8 = (f32[8,1,16,64,128]{4,3,2,1,0:T(8,128)S(1)}, f32[8,1,16,64,128]{4,3,2,1,0:T(8,128)}, u32[]{:S(2)}) copy-start(f32[8,1,16,64,128]{4,3,2,1,0:T(8,128)} %copy-done.7) | copy-start | bytes 12582916
  174.8 6.7 %copy-start.57 = (f32[16]{0:T(128)S(1)}, f32[16]{0:T(128)}, u32[]{:S(2)}) copy-start(f32[16]{0:T(128)} %get-tuple-element.115) | copy-start | bytes 196
  174.9 6.7 %copy-start.58 = (f32[16]{0:T(128)S(1)}, f32[16]{0:T(128)}, u32[]{:S(2)}) copy-start(f32[16]{0:T(128)} %get-tuple-element.116) | copy-start | bytes 196
  174.9 6.7 %copy-start.59 = (f32[16]{0:T(128)S(1)}, f32[16]{0:T(128)}, u32[]{:S(2)}) copy-start(f32[16]{0:T(128)} %get-tuple-element.117) | copy-start | bytes 196
  174.9 6.7 %copy-start.60 = (f32[16]{0:T(128)S(1)}, f32[16]{0:T(128)}, u32[]{:S(2)}) copy-start(f32[16]{0:T(128)} %get-tuple-element.118) | copy-start | bytes 196
  181.5 8.6 %copy-start.3 = (f32[128,8,8,128]{3,2,1,0:T(8,128)S(1)}, f32[128,8,8,128]{3,2,1,0:T(8,128)}, u32[]{:S(2)}) copy-start(f32[128,8,8,128]{3,2,1,0:T(8,128)} %copy-done.1) | copy-start | bytes 12582916
  183.4 29.3 %copy-start.71 = (f32[16]{0:T(128)S(1)}, f32[16]{0:T(128)}, u32[]{:S(2)}) copy-start(f32[16]{0:T(128)} %get-tuple-element.107) | copy-start | bytes 196
  183.4 29.3 %copy-start.72 = (f32[16]{0:T(128)S(1)}, f32[16]{0:T(128)}, u32[]{:S(2)}) copy-start(f32[16]{0:T(128)} %get-tuple-element.108) | copy-start | bytes 196
  183.5 29.3 %copy-start.73 = (f32[16]{0:T(128)S(1)}, f32[16]{0:T(128)}, u32[]{:S(2)}) copy-start(f32[16]{0:T(128)} %get-tuple-element.109) | copy-start | bytes 196
  183.5 29.3 %copy-start.74 = (f32[16]{0:T(128)S(1)}, f32[16]{0:T(128)}, u32[]{:S(2)}) copy-start(f32[16]{0:T(128)} %get-tuple-element.110) | copy-start | bytes 196
  183.5 29.3 %copy-start.75 = (f32[16]{0:T(128)S(1)}, f32[16]{0:T(128)}, u32[]{:S(2)}) copy-start(f32[16]{0:T(128)} %get-tuple-element.111) | copy-start | bytes 196
  183.5 29.3 %copy-start.76 = (f32[16]{0:T(128)S(1)}, f32[16]{0:T(128)}, u32[]{:S(2)}) copy-start(f32[16]{0:T(128)} %get-tuple-element.112) | copy-start | bytes 196
  183.5 29.3 %copy-start.77 = (f32[16]{0:T(128)S(1)}, f32[16]{0:T(128)}, u32[]{:S(2)}) copy-start(f32[16]{0:T(128)} %get-tuple-element.113) | copy-start | bytes 196
  183.5 29.3 %copy-start.78 = (f32[16]{0:T(128)S(1)}, f32[16]{0:T(128)}, u32[]{:S(2)}) copy-start(f32[16]{0:T(128)} %get-tuple-element.114) | copy-start | bytes 196
  183.5 29.3 %copy-start.87 = (f32[16]{0:T(128)S(1)}, f32[16]{0:T(128)}, u32[]{:S(2)}) copy-start(f32[16]{0:T(128)} %exp.181) | copy-start | bytes 196
  183.5 10.9 %collective-permute-start.12 = (f32[1,16,64,128]{3,2,1,0:T(8,128)S(1)}, f32[1,16,64,128]{3,2,1,0:T(8,128)S(1)}, u32[]{:S(2)}, u32[]{:S(2)}) collective-permute-start(f32[1,16,64,128]{3,2,1,0:T(8,128)S(1)} %fusion.112), channel_id=1, source_target_pairs={{96,0},{104,8},{112,16},{120,24},{97,1},{105,9},{113,17},{121,25},... | collective-permute-start | bytes 1572872 | tf_op jit(solution)/shard_map/ppermute | solution.py:45
  184.2 13.8 %collective-permute-start.13 = (f32[1,16,64,128]{3,2,1,0:T(8,128)S(1)}, f32[1,16,64,128]{3,2,1,0:T(8,128)S(1)}, u32[]{:S(2)}, u32[]{:S(2)}) collective-permute-start(f32[1,16,64,128]{3,2,1,0:T(8,128)S(1)} %fusion.112), channel_id=1, source_target_pairs={{64,0},{96,32},{72,8},{104,40},{80,16},{112,48},{88,24},{120,56},{... | collective-permute-start | bytes 1572872 | tf_op jit(solution)/shard_map/ppermute | solution.py:45
  185.5 27.2 %collective-permute-start.14 = (f32[1,16,64,128]{3,2,1,0:T(8,128)S(1)}, f32[1,16,64,128]{3,2,1,0:T(8,128)S(1)}, u32[]{:S(2)}, u32[]{:S(2)}) collective-permute-start(f32[1,16,64,128]{3,2,1,0:T(8,128)S(1)} %fusion.112), channel_id=1, source_target_pairs={{32,0},{64,32},{96,64},{40,8},{72,40},{104,72},{48,16},{80,48},{11... | collective-permute-start | bytes 1572872 | tf_op jit(solution)/shard_map/ppermute | solution.py:45
  190.1 24.9 %copy-start.4 = (f32[1024,1024]{0,1:T(8,128)S(1)}, f32[1024,1024]{0,1:T(8,128)}, u32[]{:S(2)}) copy-start(f32[1024,1024]{0,1:T(8,128)} %get-tuple-element.84) | copy-start | bytes 12582916
  190.1 24.9 %copy-start.37 = (f32[2,8,8,128]{3,1,2,0:T(8,128)S(1)}, f32[2,8,8,128]{3,1,2,0:T(8,128)}, u32[]{:S(2)}) copy-start(f32[2,8,8,128]{3,1,2,0:T(8,128)} %copy-done.36) | copy-start | bytes 196612
  218.2 5.1 %copy-start.48 = (f32[8,128,1,16]{1,3,0,2:T(8,128)S(1)}, f32[8,128,1,16]{1,3,0,2:T(8,128)}, u32[]{:S(2)}) copy-start(f32[8,128,1,16]{1,3,0,2:T(8,128)} %convolution_bitcast_fusion.3) | copy-start | bytes 196612
  (40 other events, 105.1 us)
